TPU v7x, 1024 devices: a whole 8x8x8 slice. The times are simulated.
1024 devices in a mesh: row: 16 (over x, core), col: 64 (over z, y).
Axes of the slice: x: 8, y: 8, z: 8, core: 2. Of those that a mesh axis runs over, the one named last changes fastest.
Arguments:
- states: bfloat16 [131072, 384], P(('row', 'col')), may hold values from -6 to 6
- mix_weight: bfloat16 [384, 384], replicated, may hold values from -0.3125 to 0.3125
- coherence: bfloat16 [16, 64, 32, 128, 128], P('row', 'col'), may hold values from -0.125 to 0.125
- block_row: int32 [16, 64, 32], P('row', 'col'), may hold values from 0 to 15, as said below
- block_col: int32 [16, 64, 32], P('row', 'col'), may hold values from 0 to 15
- block_count: int32 [16, 64], P('row', 'col'), may hold values from 8 to 32, as said below
- gain: float32 [384], replicated, may hold values from 0.5 to 1.5
- bias: float32 [384], replicated, may hold values from -3 to 3
Outputs:
- linked: bfloat16 [131072, 384], P(('row', 'col'))
Inputs may be any that keep to these rules, and one draw needn't show every extreme that they name: `block_count`: no device has more than 32 live slots, and some device has exactly 32. `block_row`: at most 2 of one device's slots name any one block row; in each column group some block row is named by 2 live slots of every device.
All inputs are finite; a program needn't handle non-finite values.
Results may differ from a plain program's by a relative error of at most 0.014.
Values may be sent and summed in bfloat16 or wider, within the bound.
No kernel may reach another device: no remote copies, remote signals or barrier semaphores. Data moves between devices by JAX's collectives and lax.ppermute only.
A program may use at most 32 MiB of HBM per device.

v0:
```python
import jax
import jax.numpy as jnp
from jax import lax
from jax.sharding import PartitionSpec as P

ITERS = 2


def normalize(hidden, coupled, gain, bias):
    summed_in = hidden.astype(jnp.float32) + coupled
    mean_value = jnp.mean(summed_in, axis=-1, keepdims=True)
    centered = summed_in - mean_value
    variance = jnp.mean(centered * centered, axis=-1, keepdims=True)
    return (centered * lax.rsqrt(variance + 1e-05) * gain + bias).astype(jnp.bfloat16)


def to_grid(values):
    return lax.all_to_all(values, "col", split_axis=0, concat_axis=0, tiled=True)


def seat_layout(blocks, row_ids, col_ids, live_count, row_groups, seats_per_row):
    slot_total = row_ids.shape[0]
    block_len = blocks.shape[1]
    slot_ids = jnp.arange(slot_total, dtype=jnp.int32)
    live_mask = slot_ids < live_count
    earlier = (
        (row_ids[:, None] == row_ids[None, :])
        & (slot_ids[None, :] < slot_ids[:, None])
        & live_mask[None, :]
    )
    rank_in_row = jnp.sum(earlier.astype(jnp.int32), axis=1)
    seat_total = row_groups * seats_per_row
    seat_index = jnp.where(live_mask, row_ids * seats_per_row + rank_in_row, seat_total)
    seat_blocks = (
        jnp.zeros((seat_total, block_len, block_len), blocks.dtype)
        .at[seat_index]
        .set(blocks, mode="drop")
    )
    seat_cols = jnp.zeros((seat_total,), jnp.int32).at[seat_index].set(col_ids, mode="drop")
    return (
        seat_blocks.reshape(row_groups, seats_per_row, block_len, block_len),
        seat_cols.reshape(row_groups, seats_per_row),
    )


def seat_product(seat_blocks, seat_cols, pieces_all):
    pieces = pieces_all[seat_cols]
    return jnp.einsum("skab,skbh->sah", seat_blocks, pieces, preferred_element_type=jnp.float32)


def couple(grid_mixed, prepared):
    gathered = lax.all_gather(grid_mixed, "row", axis=0, tiled=True)
    row_groups = lax.axis_size("row")
    block_len = grid_mixed.shape[0]
    feat_width = grid_mixed.shape[1]
    pieces_all = gathered.reshape(row_groups, block_len, feat_width)
    seat_blocks, seat_cols = prepared
    flat_sum = seat_product(seat_blocks, seat_cols, pieces_all).reshape(
        row_groups * block_len, feat_width
    )
    return lax.psum_scatter(
        flat_sum.astype(jnp.bfloat16), "row", scatter_dimension=0, tiled=True
    ).astype(jnp.float32)


def body(states, mix_weight, coherence, block_row, block_col, block_count, gain, bias):
    blocks = coherence[0, 0]
    row_ids = block_row[0, 0]
    col_ids = block_col[0, 0]
    live_count = block_count[0, 0]
    row_groups = lax.axis_size("row")
    slot_total = row_ids.shape[0]
    seats_per_row = max(2, (slot_total + row_groups - 1) // row_groups)
    prepared = seat_layout(blocks, row_ids, col_ids, live_count, row_groups, seats_per_row)
    hidden = states
    for iteration in range(ITERS):
        mixed = jnp.dot(hidden, mix_weight, preferred_element_type=jnp.float32).astype(jnp.bfloat16)
        coupled = couple(to_grid(mixed), prepared)
        coupled = lax.all_to_all(
            coupled.astype(jnp.bfloat16), "col", split_axis=0, concat_axis=0, tiled=True
        ).astype(coupled.dtype)
        hidden = normalize(hidden, coupled, gain, bias)
    return hidden


def solution(mesh):
    placed = (
        P(("row", "col"), None),
        P(),
        P("row", "col", None, None, None),
        P("row", "col", None),
        P("row", "col", None),
        P("row", "col"),
        P(),
        P(),
    )
    return jax.shard_map(
        body, mesh=mesh, in_specs=placed, out_specs=P(("row", "col"), None), check_vma=False
    )
```

profile of v0, /device:TPU:7, one launch (start us, length us, event | category | flops | bytes accessed | tf_op | source)
XLA Modules:
  0.0 335.8 jit_solution(17074291277676075526)
XLA Ops:
  6.5 0.0 copy-start
  6.5 0.0 all-gather.3.cloned.1.call-start
  6.5 1.0 copy-done
  7.5 1.1 convolution_convert_fusion.1
  8.7 34.3 %all_to_all.42 = bf16[64,2,384]{2,1,0:T(2,128)(2,1)S(1)} all-to-all(bf16[64,2,384]{2,1,0:T(2,128)(2,1)S(1)} %all_to_all.28), channel_id=1, replica_groups=mesh['row'=16,'col'=64] {'col'}, dimensions={0} | all-to-all | bytes 196608 | tf_op jit(solution)/shard_map/all_to_all | solution.py:18
  43.0 0.7 all_to_all.30
  43.7 0.0 all-gather.3.cloned.1.call-update
  43.7 0.0 reduce-scatter.3.cloned.1.call-start
  44.4 0.9 convert_reduce_fusion
  45.3 0.7 fusion.4
  46.0 0.8 scatter_custom_fusion.1
  46.8 0.1 reshape.128
  46.9 0.1 reshape.134
  47.0 0.2 broadcast_in_dim.6
  47.2 3.6 %scatter_fusion = bf16[32,128,128]{2,1,0:T(8,128)(2,1)S(1)} fusion(bf16[32,128,128]{2,1,0:T(8,128)(2,1)S(1)} %broadcast_in_dim.6, s32[32]{0:T(128)S(1)} %fusion.4, bf16[32,128,128]{2,1,0:T(8,128)(2,1)} %bitcast.51), kind=kCustom, calls=%fused_computation.2 | custom fusion | bytes 3145856 | tf_op jit(solution)/shard_map/scatter | solution.py:37
  50.8 29.8 %all-gather.3.cloned.1.call-done = bf16[2048,384]{1,0:T(8,128)(2,1)} async-done(((bf16[128,384]{1,0:T(8,128)(2,1)}), bf16[2048,384]{1,0:T(8,128)(2,1)}) %all-gather.3.cloned.1.call-update) | async-done | bytes 1572880 | tf_op jit(solution)/shard_map/all_gather | solution.py:52
  80.6 4.1 %gather_fusion = bf16[32,128,384]{2,1,0:T(8,128)(2,1)} fusion(bf16[16,128,384]{2,1,0:T(8,128)(2,1)} %bitcast.47, s32[1024]{0:T(1024)S(1)} %pad_clamp_fusion), kind=kCustom, calls=%fused_computation | custom fusion | bytes 6291584 | tf_op jit(solution)/shard_map/gather | solution.py:47
  84.7 0.0 copy-start.1
  84.7 0.0 copy-start.2
  84.7 0.0 copy-start.3
  84.7 3.8 %bitcast_convert_fusion.1 = bf16[16,128,384]{2,1,0:T(8,128)(2,1)} fusion(bf16[16,2,128,128]{3,2,1,0:T(8,128)(2,1)S(1)} %bitcast.43, bf16[16,2,128,384]{3,2,1,0:T(8,128)(2,1)} %bitcast.46), kind=kOutput, calls=%fused_computation.5 | convolution fusion | flops 403439616 | bytes 5767168 | tf_op jit(solution)/shard_map/skab,skbh->sah/dot_general | solution.py:48
  88.5 0.0 reduce-scatter.3.cloned.1.call-update
  88.5 0.0 all-gather.5.cloned.1.call-start
  88.5 63.9 %reduce-scatter.3.cloned.1.call-done = bf16[128,384]{1,0:T(8,128)(2,1)} async-done(((bf16[2048,384]{1,0:T(8,128)(2,1)}), bf16[128,384]{1,0:T(8,128)(2,1)}) %reduce-scatter.3.cloned.1.call-update) | async-done | bytes 98320 | tf_op jit(solution)/shard_map/reduce_scatter | solution.py:61
  152.4 0.9 all_to_all.31
  153.3 25.0 %all_to_all.43 = bf16[64,2,384]{2,1,0:T(2,128)(2,1)S(1)} all-to-all(bf16[64,2,384]{2,1,0:T(2,128)(2,1)S(1)} %all_to_all.31), channel_id=1, replica_groups=mesh['row'=16,'col'=64] {'col'}, dimensions={0} | all-to-all | bytes 196608 | tf_op jit(solution)/shard_map/all_to_all | solution.py:79
  178.4 0.0 copy-done.1
  178.4 0.1 fusion
  178.5 0.2 multiply_reduce_fusion.1
  178.7 0.0 copy-done.2
  178.7 0.0 copy-done.3
  178.7 0.1 add_convert_fusion.1
  178.8 0.2 convolution_convert_fusion
  179.1 15.2 %all_to_all.44 = bf16[64,2,384]{2,1,0:T(2,128)(2,1)S(1)} all-to-all(bf16[64,2,384]{2,1,0:T(2,128)(2,1)S(1)} %all_to_all.33), channel_id=1, replica_groups=mesh['row'=16,'col'=64] {'col'}, dimensions={0} | all-to-all | bytes 196608 | tf_op jit(solution)/shard_map/all_to_all | solution.py:18
  194.3 0.7 all_to_all.35
  194.9 0.0 all-gather.5.cloned.1.call-update
  195.0 0.0 reduce-scatter.5.cloned.1.call-start
  195.0 35.4 %all-gather.5.cloned.1.call-done = bf16[2048,384]{1,0:T(8,128)(2,1)} async-done(((bf16[128,384]{1,0:T(8,128)(2,1)}), bf16[2048,384]{1,0:T(8,128)(2,1)}) %all-gather.5.cloned.1.call-update) | async-done | bytes 1572880 | tf_op jit(solution)/shard_map/all_gather | solution.py:52
  230.4 4.1 %gather_fusion.1 = bf16[32,128,384]{2,1,0:T(8,128)(2,1)} fusion(bf16[16,128,384]{2,1,0:T(8,128)(2,1)} %bitcast.48, s32[1024]{0:T(1024)S(1)} %pad_clamp_fusion), kind=kCustom, calls=%fused_computation.1 | custom fusion | bytes 6291584 | tf_op jit(solution)/shard_map/gather | solution.py:47
  234.5 3.7 %bitcast_convert_fusion = bf16[16,128,384]{2,1,0:T(8,128)(2,1)} fusion(bf16[16,2,128,128]{3,2,1,0:T(8,128)(2,1)S(1)} %bitcast.44, bf16[16,2,128,384]{3,2,1,0:T(8,128)(2,1)} %bitcast.45), kind=kOutput, calls=%fused_computation.4 | convolution fusion | flops 403439616 | bytes 5767168 | tf_op jit(solution)/shard_map/skab,skbh->sah/dot_general | solution.py:48
  238.2 0.0 reduce-scatter.5.cloned.1.call-update
  238.3 63.9 %reduce-scatter.5.cloned.1.call-done = bf16[128,384]{1,0:T(8,128)(2,1)} async-done(((bf16[2048,384]{1,0:T(8,128)(2,1)}), bf16[128,384]{1,0:T(8,128)(2,1)}) %reduce-scatter.5.cloned.1.call-update) | async-done | bytes 98320 | tf_op jit(solution)/shard_map/reduce_scatter | solution.py:61
  302.2 0.9 all_to_all.36
  303.1 25.0 %all_to_all.45 = bf16[64,2,384]{2,1,0:T(2,128)(2,1)S(1)} all-to-all(bf16[64,2,384]{2,1,0:T(2,128)(2,1)S(1)} %all_to_all.36), channel_id=1, replica_groups=mesh['row'=16,'col'=64] {'col'}, dimensions={0} | all-to-all | bytes 196608 | tf_op jit(solution)/shard_map/all_to_all | solution.py:79
  328.1 0.1 fusion.1
  328.3 0.2 multiply_reduce_fusion
  328.5 0.8 add_convert_fusion
  (11 shorter events, 0.2 us)
Async XLA Ops:
  6.5 1.0 copy-start
  6.5 74.1 %all-gather.3.cloned.1.call-start = ((), (), s32[]{:S(2)}) async-start(), calls=%async_computation.6 | async-start | bytes 1671168 | tf_op jit(solution)/shard_map/all_gather | solution.py:52
  43.7 108.7 %reduce-scatter.3.cloned.1.call-start = ((), (), s32[]{:S(2)}) async-start(), calls=%async_computation.7 | async-start | bytes 1671168 | tf_op jit(solution)/shard_map/reduce_scatter | solution.py:61
  84.7 93.7 %copy-start.1 = (bf16[128,384]{1,0:T(8,128)(2,1)S(1)}, bf16[128,384]{1,0:T(8,128)(2,1)}, u32[]{:S(2)}) copy-start(bf16[128,384]{1,0:T(8,128)(2,1)} %param.8) | copy-start | bytes 294916
  84.7 94.0 %copy-start.2 = (f32[384]{0:T(512)S(1)}, f32[384]{0:T(512)}, u32[]{:S(2)}) copy-start(f32[384]{0:T(512)} %param.15) | copy-start | bytes 4612
  84.7 94.0 %copy-start.3 = (f32[384]{0:T(512)S(1)}, f32[384]{0:T(512)}, u32[]{:S(2)}) copy-start(f32[384]{0:T(512)} %param.14) | copy-start | bytes 4612
  88.5 141.9 %all-gather.5.cloned.1.call-start = ((), (), s32[]{:S(2)}) async-start(), calls=%async_computation.8 | async-start | bytes 1671168 | tf_op jit(solution)/shard_map/all_gather | solution.py:52
  195.0 107.2 %reduce-scatter.5.cloned.1.call-start = ((), (), s32[]{:S(2)}) async-start(), calls=%async_computation.9 | async-start | bytes 1671168 | tf_op jit(solution)/shard_map/reduce_scatter | solution.py:61
Sparse Core Ops, SparseCore 0:
  43.8 36.7 all-gather.2
  88.6 63.7 reduce-scatter.2
  195.1 35.2 all-gather.4
  238.4 63.7 reduce-scatter.4
where the time goes:
time: 336 us
  waiting for transfers between devices  193 us (57%)
  blocking collectives  99.5 us (30%)
  local copies, waits for them, and re-layouts  17.3 us (5%)
  between operations  13.9 us (4%)
  matrix products  8.82 us (3%)
    reduce_scatter x2, waiting for transfers between devices, couple(): lax.psum_scatter(flat_sum.astype(jnp.bfloat16), 'row', scatter_dimension=...  128 us
    all_gather x2, waiting for transfers between devices, couple(): gathered = lax.all_gather(grid_mixed, 'row', axis=0, tiled=True)  65.2 us
    all_to_all x2, blocking collectives, body(): lax.all_to_all(coupled.astype(jnp.bfloat16), 'col', split_axis=0, concat_...  50 us
    all_to_all x2, blocking collectives, to_grid(): lax.all_to_all(values, 'col', split_axis=0, concat_axis=0, tiled=True)  49.5 us
    gather x2, local copies, waits for them, and re-layouts, seat_product(): pieces = pieces_all[seat_cols]  8.11 us
    dot_general x2, matrix products, seat_product(): jnp.einsum('skab,skbh->sah', seat_blocks, pieces, preferred_element_type=...  7.51 us
  transfers between devices with their start and end apart: 4, of which 4 were waited for; matrix products, arithmetic and copies ran while one was open for 2% of the time, Pallas kernels for 0%

commit v1 on v0

--- a/solution.py
+++ b/solution.py
@@ -43,24 +43,13 @@
     )
 
 
-def seat_product(seat_blocks, seat_cols, pieces_all):
-    pieces = pieces_all[seat_cols]
-    return jnp.einsum("skab,skbh->sah", seat_blocks, pieces, preferred_element_type=jnp.float32)
-
-
-def couple(grid_mixed, prepared):
-    gathered = lax.all_gather(grid_mixed, "row", axis=0, tiled=True)
-    row_groups = lax.axis_size("row")
-    block_len = grid_mixed.shape[0]
-    feat_width = grid_mixed.shape[1]
-    pieces_all = gathered.reshape(row_groups, block_len, feat_width)
-    seat_blocks, seat_cols = prepared
-    flat_sum = seat_product(seat_blocks, seat_cols, pieces_all).reshape(
-        row_groups * block_len, feat_width
+def couple(grid_mixed, owned_blocks, owned_cols):
+    pieces_all = lax.all_gather(grid_mixed, "row", axis=0, tiled=False)
+    pieces = pieces_all[owned_cols]
+    per_source = jnp.einsum(
+        "rsab,rsbh->rah", owned_blocks, pieces, preferred_element_type=jnp.float32
     )
-    return lax.psum_scatter(
-        flat_sum.astype(jnp.bfloat16), "row", scatter_dimension=0, tiled=True
-    ).astype(jnp.float32)
+    return jnp.sum(per_source.astype(jnp.bfloat16).astype(jnp.float32), axis=0)
 
 
 def body(states, mix_weight, coherence, block_row, block_col, block_count, gain, bias):
@@ -71,16 +60,17 @@
     row_groups = lax.axis_size("row")
     slot_total = row_ids.shape[0]
     seats_per_row = max(2, (slot_total + row_groups - 1) // row_groups)
-    prepared = seat_layout(blocks, row_ids, col_ids, live_count, row_groups, seats_per_row)
-    hidden = states
+    seat_blocks, seat_cols = seat_layout(
+        blocks, row_ids, col_ids, live_count, row_groups, seats_per_row
+    )
+    owned_blocks = lax.all_to_all(seat_blocks, "row", split_axis=0, concat_axis=0, tiled=True)
+    owned_cols = lax.all_to_all(seat_cols, "row", split_axis=0, concat_axis=0, tiled=True)
+    hidden = to_grid(states)
     for iteration in range(ITERS):
         mixed = jnp.dot(hidden, mix_weight, preferred_element_type=jnp.float32).astype(jnp.bfloat16)
-        coupled = couple(to_grid(mixed), prepared)
-        coupled = lax.all_to_all(
-            coupled.astype(jnp.bfloat16), "col", split_axis=0, concat_axis=0, tiled=True
-        ).astype(coupled.dtype)
+        coupled = couple(mixed, owned_blocks, owned_cols)
         hidden = normalize(hidden, coupled, gain, bias)
-    return hidden
+    return to_grid(hidden)
 
 
 def solution(mesh):

time: 336 us -> 185 us (0.55)
  the two profiles are of different devices: /device:TPU:7 before, /device:TPU:6 now
where the time goes in v1:
time: 185 us
  waiting for transfers between devices  64.7 us (35%)
  blocking collectives  62 us (34%)
  local copies, waits for them, and re-layouts  17 us (9%)
  starting transfers between devices  14.9 us (8%)
  between operations  14.3 us (8%)
  matrix products  8.01 us (4%)
  other arithmetic  3.91 us (2%)
    all_to_all x2, blocking collectives, to_grid(): lax.all_to_all(values, 'col', split_axis=0, concat_axis=0, tiled=True)  62 us
    all_gather x2, waiting for transfers between devices, couple(): pieces_all = lax.all_gather(grid_mixed, 'row', axis=0, tiled=False)  53.9 us
    all_to_all x1, waiting for transfers between devices, body(): lax.all_to_all(seat_blocks, 'row', split_axis=0, concat_axis=0, tiled=True)  10.8 us
    all_to_all x1, starting transfers between devices, body(): lax.all_to_all(seat_blocks, 'row', split_axis=0, concat_axis=0, tiled=True)  7.6 us
    all_to_all x1, starting transfers between devices, body(): lax.all_to_all(seat_cols, 'row', split_axis=0, concat_axis=0, tiled=True)  7.25 us
    gather x2, local copies, waits for them, and re-layouts, couple(): pieces = pieces_all[owned_cols]  5.28 us
    dot_general x2, matrix products, couple(): jnp.einsum('rsab,rsbh->rah', owned_blocks, pieces, preferred_element_type...  5.26 us
    scatter x1, local copies, waits for them, and re-layouts, seat_layout(): seat_blocks = jnp.zeros((seat_total, block_len, block_len), blocks.dtype)...  4.65 us
  transfers between devices with their start and end apart: 4, of which 3 were waited for; matrix products, arithmetic and copies ran while one was open for 6% of the time, Pallas kernels for 0%

profile of v1, /device:TPU:6, one launch (start us, length us, event | category | flops | bytes accessed | tf_op | source)
XLA Modules:
  0.0 184.8 jit_solution(14115592982561556402)
XLA Ops:
  6.5 0.0 copy-start
  6.5 0.0 all-gather.5.cloned.1.call-start
  6.5 1.0 all_to_all.25
  7.5 35.7 %all_to_all.38 = bf16[64,2,384]{2,1,0:T(2,128)(2,1)S(1)} all-to-all(bf16[64,2,384]{2,1,0:T(2,128)(2,1)S(1)} %all_to_all.25), channel_id=1, replica_groups=mesh['row'=16,'col'=64] {'col'}, dimensions={0} | all-to-all | bytes 196608 | tf_op jit(solution)/shard_map/all_to_all | solution.py:18
  43.2 0.0 copy-done
  43.2 0.0 copy-start.2
  43.2 0.9 convolution_convert_fusion.1
  44.1 0.0 all-gather.5.cloned.1.call-update
  44.8 0.9 convert_reduce_fusion.2
  45.7 0.7 fusion.7
  46.4 0.8 scatter_custom_fusion.1
  47.2 0.7 all_to_all.29
  47.9 7.3 %all-to-all-start.2 = ((s32[16,1,2]{2,1,0:T(1,128)}), s32[16,1,2]{2,1,0:T(1,128)S(1)}, u32[]{:S(2)}, u32[]{:S(2)}) async-start(s32[16,1,2]{2,1,0:T(1,128)} %bitcast.9), calls=%async_computation.2 | async-start | bytes 16384 | tf_op jit(solution)/shard_map/all_to_all | solution.py:67
  55.1 1.2 broadcast_in_dim.6
  56.3 4.6 %scatter_fusion = bf16[32,128,128]{2,1,0:T(8,128)(2,1)} fusion(bf16[32,128,128]{2,1,0:T(8,128)(2,1)} %broadcast_in_dim.6, s32[32]{0:T(128)S(1)} %fusion.7, bf16[32,128,128]{2,1,0:T(8,128)(2,1)} %bitcast.51), kind=kCustom, calls=%fused_computation.2 | custom fusion | bytes 3145856 | tf_op jit(solution)/shard_map/scatter | solution.py:37
  61.0 0.0 all-to-all-done.2
  61.0 0.0 copy-done.2
  61.0 7.6 %all-to-all-start.1 = ((bf16[16,2,128,128]{3,2,1,0:T(8,128)(2,1)}), bf16[16,2,128,128]{3,2,1,0:T(8,128)(2,1)}, u32[]{:S(2)}, u32[]{:S(2)}) async-start(bf16[16,2,128,128]{3,2,1,0:T(8,128)(2,1)} %bitcast.6), calls=%async_computation.1 | async-start | bytes 2097152 | tf_op jit(solution)/shard_map/all_to_all | solution.py:66
  68.6 0.0 all-gather.7.cloned.1.call-start
  68.7 0.1 copy.17
  68.7 0.1 copy.18
  68.8 0.1 reshape.225
  68.9 13.5 %all-gather.5.cloned.1.call-done = bf16[2048,384]{1,0:T(8,128)(2,1)} async-done(((bf16[128,384]{1,0:T(8,128)(2,1)}), bf16[2048,384]{1,0:T(8,128)(2,1)}) %all-gather.5.cloned.1.call-update) | async-done | bytes 1572880 | tf_op jit(solution)/shard_map/all_gather | solution.py:47
  82.4 2.6 %gather_fusion = bf16[32,128,384]{2,1,0:T(8,128)(2,1)S(1)} fusion(bf16[16,128,384]{2,1,0:T(8,128)(2,1)} %bitcast.49, s32[1024]{0:T(1024)S(1)} %pad_clamp_fusion), kind=kCustom, calls=%fused_computation | custom fusion | bytes 6291584 | tf_op jit(solution)/shard_map/gather | solution.py:48
  85.1 0.0 copy-start.5
  85.1 0.0 copy-start.6
  85.1 10.8 %all-to-all-done.1 = bf16[16,2,128,128]{3,2,1,0:T(8,128)(2,1)} async-done(((bf16[16,2,128,128]{3,2,1,0:T(8,128)(2,1)}), bf16[16,2,128,128]{3,2,1,0:T(8,128)(2,1)}, u32[]{:S(2)}, u32[]{:S(2)}) %all-to-all-start.1) | async-done | bytes 1048608 | tf_op jit(solution)/shard_map/all_to_all | solution.py:66
  95.8 2.6 %convert_reduce_fusion.1 = f32[128,384]{1,0:T(8,128)} fusion(bf16[16,2,128,128]{3,2,1,0:T(8,128)(2,1)} %all-to-all-done.1, bf16[16,2,128,384]{3,2,1,0:T(8,128)(2,1)S(1)} %bitcast.47), kind=kOutput, calls=%fused_computation.7 | convolution fusion | flops 404963328 | bytes 4390912 | tf_op jit(solution)/shard_map/rsab,rsbh->rah/dot_general | solution.py:49
  98.5 1.0 reduce_sum.72
  99.5 0.0 copy-start.1
  99.5 0.2 fusion.6
  99.7 0.0 copy-start.3
  99.7 0.1 div.16
  99.8 0.3 multiply_reduce_fusion.1
  100.1 0.0 copy-start.4
  100.2 0.1 rsqrt.21
  100.3 0.0 copy-done.5
  100.3 0.0 copy-done.6
  100.3 1.9 %convolution_convert_fusion = bf16[128,384]{1,0:T(8,128)(2,1)} fusion(bf16[384,384]{1,0:T(8,128)(2,1)S(1)} %copy-done, f32[128,384]{1,0:T(8,128)} %convert_reduce_fusion.1, bf16[128,384]{1,0:T(8,128)(2,1)} %copy-done.2, f32[384]{0:T(512)S(1)} %copy-done.5, f32[384]{0:T(512)S(1)} %copy-done.6, f32[128]{0:T(128)S(1)} %rsqrt.21, f32[128]{0:T(128)S(1)} %div.16), kind=kOutput, calls=%fused_computation.8 | convolution fusion | flops 38141952 | bytes 692224 | tf_op jit(solution)/shard_map/dot_general | solution.py:70
  102.2 0.0 all-gather.7.cloned.1.call-update
  102.2 40.4 %all-gather.7.cloned.1.call-done = bf16[2048,384]{1,0:T(8,128)(2,1)} async-done(((bf16[128,384]{1,0:T(8,128)(2,1)}), bf16[2048,384]{1,0:T(8,128)(2,1)}) %all-gather.7.cloned.1.call-update) | async-done | bytes 1572880 | tf_op jit(solution)/shard_map/all_gather | solution.py:47
  142.7 0.0 copy-done.1
  142.7 0.0 copy-done.3
  142.7 0.0 copy-done.4
  142.7 2.6 %gather_fusion.1 = bf16[32,128,384]{2,1,0:T(8,128)(2,1)S(1)} fusion(bf16[16,128,384]{2,1,0:T(8,128)(2,1)} %bitcast.50, s32[1024]{0:T(1024)S(1)} %pad_clamp_fusion), kind=kCustom, calls=%fused_computation.1 | custom fusion | bytes 6291584 | tf_op jit(solution)/shard_map/gather | solution.py:48
  145.3 2.6 %convert_reduce_fusion = f32[128,384]{1,0:T(8,128)} fusion(bf16[16,2,128,128]{3,2,1,0:T(8,128)(2,1)} %all-to-all-done.1, bf16[16,2,128,384]{3,2,1,0:T(8,128)(2,1)S(1)} %bitcast.48), kind=kOutput, calls=%fused_computation.6 | convolution fusion | flops 404963328 | bytes 4390912 | tf_op jit(solution)/shard_map/rsab,rsbh->rah/dot_general | solution.py:49
  147.9 1.0 reduce_sum.76
  149.0 1.4 fusion.10
  150.3 0.2 multiply_reduce_fusion
  150.6 0.2 add_convert_fusion
  150.8 26.4 %all_to_all.39 = bf16[64,2,384]{2,1,0:T(2,128)(2,1)S(1)} all-to-all(bf16[64,2,384]{2,1,0:T(2,128)(2,1)S(1)} %add_convert_fusion), channel_id=1, replica_groups=mesh['row'=16,'col'=64] {'col'}, dimensions={0} | all-to-all | bytes 196608 | tf_op jit(solution)/shard_map/all_to_all | solution.py:18
  177.2 0.7 all_to_all.33
  (8 shorter events, 0.1 us)
Async XLA Ops:
  6.5 36.7 %copy-start = (bf16[384,384]{1,0:T(8,128)(2,1)S(1)}, bf16[384,384]{1,0:T(8,128)(2,1)}, u32[]{:S(2)}) copy-start(bf16[384,384]{1,0:T(8,128)(2,1)} %param.9) | copy-start | bytes 884740
  6.5 75.9 %all-gather.5.cloned.1.call-start = ((), (), s32[]{:S(2)}) async-start(), calls=%async_computation.4 | async-start | bytes 1671168 | tf_op jit(solution)/shard_map/all_gather | solution.py:47
  43.2 17.8 %copy-start.2 = (bf16[128,384]{1,0:T(8,128)(2,1)}, bf16[128,384]{1,0:T(8,128)(2,1)S(1)}, u32[]{:S(2)}) copy-start(bf16[128,384]{1,0:T(8,128)(2,1)S(1)} %all_to_all.28) | copy-start | bytes 294916
  47.9 13.1 %all-to-all-start.2 = ((s32[16,1,2]{2,1,0:T(1,128)}), s32[16,1,2]{2,1,0:T(1,128)S(1)}, u32[]{:S(2)}, u32[]{:S(2)}) async-start(s32[16,1,2]{2,1,0:T(1,128)} %bitcast.9), calls=%async_computation.2 | async-start | bytes 16384 | tf_op jit(solution)/shard_map/all_to_all | solution.py:67
  61.0 34.8 %all-to-all-start.1 = ((bf16[16,2,128,128]{3,2,1,0:T(8,128)(2,1)}), bf16[16,2,128,128]{3,2,1,0:T(8,128)(2,1)}, u32[]{:S(2)}, u32[]{:S(2)}) async-start(bf16[16,2,128,128]{3,2,1,0:T(8,128)(2,1)} %bitcast.6), calls=%async_computation.1 | async-start | bytes 2097152 | tf_op jit(solution)/shard_map/all_to_all | solution.py:66
  68.6 74.0 %all-gather.7.cloned.1.call-start = ((), (), s32[]{:S(2)}) async-start(), calls=%async_computation.5 | async-start | bytes 1671168 | tf_op jit(solution)/shard_map/all_gather | solution.py:47
  85.1 15.2 %copy-start.5 = (f32[384]{0:T(512)S(1)}, f32[384]{0:T(512)}, u32[]{:S(2)}) copy-start(f32[384]{0:T(512)} %param.15) | copy-start | bytes 4612
  85.1 15.2 %copy-start.6 = (f32[384]{0:T(512)S(1)}, f32[384]{0:T(512)}, u32[]{:S(2)}) copy-start(f32[384]{0:T(512)} %param.14) | copy-start | bytes 4612
  99.5 43.2 %copy-start.1 = (f32[64,2,384]{2,1,0:T(2,128)}, f32[64,2,384]{2,1,0:T(2,128)S(1)}, u32[]{:S(2)}) copy-start(f32[64,2,384]{2,1,0:T(2,128)S(1)} %reduce_sum.72) | copy-start | bytes 589828
  99.7 43.0 %copy-start.3 = (f32[64,2]{1,0:T(8,128)}, f32[64,2]{1,0:T(8,128)S(1)}, u32[]{:S(2)}) copy-start(f32[64,2]{1,0:T(8,128)S(1)} %broadcast_multiply_fusion.1) | copy-start | bytes 1540
  100.1 42.5 %copy-start.4 = (f32[64,2]{1,0:T(8,128)}, f32[64,2]{1,0:T(8,128)S(1)}, u32[]{:S(2)}) copy-start(f32[64,2]{1,0:T(8,128)S(1)} %add_rsqrt_fusion.1) | copy-start | bytes 1540
Sparse Core Ops, SparseCore 0:
  44.2 38.1 all-gather.4
  102.4 40.2 all-gather.6

commit v2 on v1

--- a/solution.py
+++ b/solution.py
@@ -15,7 +15,13 @@
 
 
 def to_grid(values):
-    return lax.all_to_all(values, "col", split_axis=0, concat_axis=0, tiled=True)
+    col_hi = lax.axis_size("cz")
+    col_lo = lax.axis_size("cy")
+    rows = values.shape[0] // (col_hi * col_lo)
+    parts = values.reshape(col_hi, col_lo, rows, values.shape[1])
+    parts = lax.all_to_all(parts, "cy", split_axis=1, concat_axis=1, tiled=True)
+    parts = lax.all_to_all(parts, "cz", split_axis=0, concat_axis=0, tiled=True)
+    return parts.reshape(values.shape)
 
 
 def seat_layout(blocks, row_ids, col_ids, live_count, row_groups, seats_per_row):
@@ -44,8 +50,12 @@
 
 
 def couple(grid_mixed, owned_blocks, owned_cols):
-    pieces_all = lax.all_gather(grid_mixed, "row", axis=0, tiled=False)
-    pieces = pieces_all[owned_cols]
+    pieces_all = lax.all_gather(grid_mixed, "rx", axis=0, tiled=False)
+    pieces_all = lax.all_gather(pieces_all, "rc", axis=0, tiled=False)
+    cores = lax.axis_size("rc")
+    chips = lax.axis_size("rx")
+    pieces_all = pieces_all.reshape((cores * chips,) + grid_mixed.shape)
+    pieces = pieces_all[(owned_cols % cores) * chips + owned_cols // cores]
     per_source = jnp.einsum(
         "rsab,rsbh->rah", owned_blocks, pieces, preferred_element_type=jnp.float32
     )
@@ -57,14 +67,14 @@
     row_ids = block_row[0, 0]
     col_ids = block_col[0, 0]
     live_count = block_count[0, 0]
-    row_groups = lax.axis_size("row")
+    row_groups = lax.axis_size(("rx", "rc"))
     slot_total = row_ids.shape[0]
     seats_per_row = max(2, (slot_total + row_groups - 1) // row_groups)
     seat_blocks, seat_cols = seat_layout(
         blocks, row_ids, col_ids, live_count, row_groups, seats_per_row
     )
-    owned_blocks = lax.all_to_all(seat_blocks, "row", split_axis=0, concat_axis=0, tiled=True)
-    owned_cols = lax.all_to_all(seat_cols, "row", split_axis=0, concat_axis=0, tiled=True)
+    owned_blocks = lax.all_to_all(seat_blocks, ("rx", "rc"), split_axis=0, concat_axis=0, tiled=True)
+    owned_cols = lax.all_to_all(seat_cols, ("rx", "rc"), split_axis=0, concat_axis=0, tiled=True)
     hidden = to_grid(states)
     for iteration in range(ITERS):
         mixed = jnp.dot(hidden, mix_weight, preferred_element_type=jnp.float32).astype(jnp.bfloat16)
@@ -74,16 +84,24 @@
 
 
 def solution(mesh):
+    chips = mesh.devices.shape[0] // 2
+    col_hi = 8 if mesh.devices.shape[1] % 8 == 0 else 1
+    fine = jax.sharding.Mesh(
+        mesh.devices.reshape(chips, 2, col_hi, mesh.devices.shape[1] // col_hi),
+        ("rx", "rc", "cz", "cy"),
+    )
+    rows = ("rx", "rc")
+    cols = ("cz", "cy")
     placed = (
-        P(("row", "col"), None),
+        P(rows + cols, None),
         P(),
-        P("row", "col", None, None, None),
-        P("row", "col", None),
-        P("row", "col", None),
-        P("row", "col"),
+        P(rows, cols, None, None, None),
+        P(rows, cols, None),
+        P(rows, cols, None),
+        P(rows, cols),
         P(),
         P(),
     )
     return jax.shard_map(
-        body, mesh=mesh, in_specs=placed, out_specs=P(("row", "col"), None), check_vma=False
+        body, mesh=fine, in_specs=placed, out_specs=P(rows + cols, None), check_vma=False
     )

time: 185 us -> 239 us (1.29)
  the two profiles are of different devices: /device:TPU:6 before, /device:TPU:2 now
where the time goes in v2:
time: 239 us; the launch traced here: 238 us
  blocking collectives  109 us (46%)
  waiting for transfers between devices  45.8 us (19%)
  starting transfers between devices  38.6 us (16%)
  local copies, waits for them, and re-layouts  19.1 us (8%)
  between operations  14.3 us (6%)
  matrix products  6.72 us (3%)
  other arithmetic  3.95 us (2%)
    all_gather x2, blocking collectives, couple(): pieces_all = lax.all_gather(grid_mixed, 'rx', axis=0, tiled=False)  77 us
    all_gather x2, waiting for transfers between devices, couple(): pieces_all = lax.all_gather(pieces_all, 'rc', axis=0, tiled=False)  32.1 us
    all_to_all x1, starting transfers between devices, to_grid(): parts = lax.all_to_all(parts, 'cz', split_axis=0, concat_axis=0, tiled=True)  16.7 us
    all_to_all x1, blocking collectives, to_grid(): parts = lax.all_to_all(parts, 'cz', split_axis=0, concat_axis=0, tiled=True)  16.6 us
    all_to_all x1, blocking collectives, to_grid(): parts = lax.all_to_all(parts, 'cy', split_axis=1, concat_axis=1, tiled=True)  15.5 us
    all_to_all x1, starting transfers between devices, to_grid(): parts = lax.all_to_all(parts, 'cy', split_axis=1, concat_axis=1, tiled=True)  7.56 us
    all_to_all x1, starting transfers between devices, body(): lax.all_to_all(seat_cols, ('rx', 'rc'), split_axis=0, concat_axis=0, tile...  7.31 us
    all_to_all x1, waiting for transfers between devices, to_grid(): parts = lax.all_to_all(parts, 'cy', split_axis=1, concat_axis=1, tiled=True)  7.15 us
  transfers between devices with their start and end apart: 6, of which 4 were waited for; matrix products, arithmetic and copies ran while one was open for 5% of the time, Pallas kernels for 0%

profile of v2, /device:TPU:2, one launch (start us, length us, event | category | flops | bytes accessed | tf_op | source)
XLA Modules:
  0.0 237.7 jit_solution(6474187607824445567)
XLA Ops:
  6.5 0.0 copy-start
  6.5 1.0 reshape.316
  7.5 0.7 copy.34
  8.2 7.6 %all-to-all-start = ((bf16[8,8,2,384]{3,2,0,1:T(2,128)(2,1)}), bf16[8,8,2,384]{3,2,0,1:T(2,128)(2,1)S(1)}, u32[]{:S(2)}, u32[]{:S(2)}) async-start(bf16[8,8,2,384]{3,2,0,1:T(2,128)(2,1)} %copy.34), calls=%async_computation | async-start | bytes 196608 | tf_op jit(solution)/shard_map/all_to_all | solution.py:22
  16.4 0.9 convert_reduce_fusion.2
  17.4 7.2 %all-to-all-done = bf16[8,8,2,384]{3,2,0,1:T(2,128)(2,1)S(1)} async-done(((bf16[8,8,2,384]{3,2,0,1:T(2,128)(2,1)}), bf16[8,8,2,384]{3,2,0,1:T(2,128)(2,1)S(1)}, u32[]{:S(2)}, u32[]{:S(2)}) %all-to-all-start) | async-done | bytes 98336 | tf_op jit(solution)/shard_map/all_to_all | solution.py:22
  24.5 0.7 copy.35
  25.2 16.7 %all-to-all-start.1 = ((bf16[8,8,2,384]{3,2,1,0:T(2,128)(2,1)}), bf16[8,8,2,384]{3,2,1,0:T(2,128)(2,1)S(1)}, u32[]{:S(2)}, u32[]{:S(2)}) async-start(bf16[8,8,2,384]{3,2,1,0:T(2,128)(2,1)} %copy.35), calls=%async_computation.1 | async-start | bytes 196608 | tf_op jit(solution)/shard_map/all_to_all | solution.py:23
  41.9 0.7 fusion.9
  42.6 0.8 scatter_custom_fusion.1
  43.4 0.7 all_to_all.26
  44.1 6.6 %all-to-all-done.1 = bf16[8,8,2,384]{3,2,1,0:T(2,128)(2,1)S(1)} async-done(((bf16[8,8,2,384]{3,2,1,0:T(2,128)(2,1)}), bf16[8,8,2,384]{3,2,1,0:T(2,128)(2,1)S(1)}, u32[]{:S(2)}, u32[]{:S(2)}) %all-to-all-start.1) | async-done | bytes 98336 | tf_op jit(solution)/shard_map/all_to_all | solution.py:23
  50.6 7.3 %all-to-all-start.3 = ((s32[16,1,2]{2,1,0:T(1,128)}), s32[16,1,2]{2,1,0:T(1,128)S(1)}, u32[]{:S(2)}, u32[]{:S(2)}) async-start(s32[16,1,2]{2,1,0:T(1,128)} %bitcast.9), calls=%async_computation.3 | async-start | bytes 16384 | tf_op jit(solution)/shard_map/all_to_all | solution.py:77
  57.9 1.2 broadcast_in_dim.6
  59.2 5.2 %scatter_fusion = bf16[32,128,128]{2,1,0:T(8,128)(2,1)} fusion(bf16[32,128,128]{2,1,0:T(8,128)(2,1)} %broadcast_in_dim.6, s32[32]{0:T(128)S(1)} %fusion.9, bf16[32,128,128]{2,1,0:T(8,128)(2,1)} %bitcast.59), kind=kCustom, calls=%fused_computation.2 | custom fusion | bytes 3145856 | tf_op jit(solution)/shard_map/scatter | solution.py:43
  64.5 0.0 copy-start.2
  64.5 0.0 all-to-all-done.3
  64.5 7.0 %all-to-all-start.2 = ((bf16[16,2,128,128]{3,2,1,0:T(8,128)(2,1)}), bf16[16,2,128,128]{3,2,1,0:T(8,128)(2,1)}, u32[]{:S(2)}, u32[]{:S(2)}) async-start(bf16[16,2,128,128]{3,2,1,0:T(8,128)(2,1)} %bitcast.6), calls=%async_computation.2 | async-start | bytes 2097152 | tf_op jit(solution)/shard_map/all_to_all | solution.py:76
  71.5 0.0 all-gather.7.cloned.1.call-start
  71.5 0.0 copy-done
  71.5 0.2 convolution_convert_fusion.1
  71.7 48.9 %all-gather = bf16[1024,384]{1,0:T(8,128)(2,1)} all-gather(bf16[128,384]{1,0:T(8,128)(2,1)S(1)} %convolution_convert_fusion.1), channel_id=2, replica_groups=mesh['rx'=8,'rc'=2,'cz'=8,'cy'=8] {'rx'}, dimensions={0}, use_global_device_ids=true | all-gather | bytes 884736 | tf_op jit(solution)/shard_map/all_gather | solution.py:53
  120.6 0.0 all-gather.7.cloned.1.call-update
  120.6 0.0 all-gather.9.cloned.1.call-start
  120.7 0.1 copy.37
  120.8 0.1 copy.38
  120.9 0.1 reshape.324
  121.0 0.0 copy-done.2
  121.0 9.6 %all-gather.7.cloned.1.call-done = bf16[16,128,384]{2,1,0:T(8,128)(2,1)} async-done(((bf16[8,128,384]{2,1,0:T(8,128)(2,1)}), bf16[16,128,384]{2,1,0:T(8,128)(2,1)}) %all-gather.7.cloned.1.call-update) | async-done | bytes 1572880 | tf_op jit(solution)/shard_map/all_gather | solution.py:54
  130.5 2.6 %gather_fusion = bf16[32,128,384]{2,1,0:T(8,128)(2,1)S(1)} fusion(bf16[16,128,384]{2,1,0:T(8,128)(2,1)} %all-gather.7.cloned.1.call-done, s32[1024]{0:T(1024)S(1)} %pad_clamp_fusion), kind=kCustom, calls=%fused_computation | custom fusion | bytes 6291584 | tf_op jit(solution)/shard_map/gather | solution.py:58
  133.2 0.0 copy-start.5
  133.2 0.0 copy-start.6
  133.2 0.0 all-to-all-done.2
  133.2 2.6 %convert_reduce_fusion.1 = f32[128,384]{1,0:T(8,128)} fusion(bf16[16,2,128,128]{3,2,1,0:T(8,128)(2,1)} %all-to-all-done.2, bf16[16,2,128,384]{3,2,1,0:T(8,128)(2,1)S(1)} %bitcast.55), kind=kOutput, calls=%fused_computation.7 | convolution fusion | flops 404963328 | bytes 4390912 | tf_op jit(solution)/shard_map/rsab,rsbh->rah/dot_general | solution.py:59
  135.9 1.0 reduce_sum.72
  136.9 0.0 copy-start.1
  136.9 0.2 fusion.6
  137.1 0.0 copy-start.3
  137.1 0.1 div.31
  137.2 0.3 multiply_reduce_fusion.1
  137.6 0.0 copy-start.4
  137.6 0.1 rsqrt.21
  137.7 0.0 copy-done.5
  137.7 0.0 copy-done.6
  137.7 1.3 convolution_convert_fusion
  139.0 28.2 %all-gather.2 = bf16[1024,384]{1,0:T(8,128)(2,1)} all-gather(bf16[128,384]{1,0:T(8,128)(2,1)S(1)} %convolution_convert_fusion), channel_id=4, replica_groups=mesh['rx'=8,'rc'=2,'cz'=8,'cy'=8] {'rx'}, dimensions={0}, use_global_device_ids=true | all-gather | bytes 884736 | tf_op jit(solution)/shard_map/all_gather | solution.py:53
  167.2 0.0 all-gather.9.cloned.1.call-update
  167.2 0.0 copy-done.1
  167.2 0.0 copy-done.3
  167.2 0.0 copy-done.4
  167.2 22.5 %all-gather.9.cloned.1.call-done = bf16[16,128,384]{2,1,0:T(8,128)(2,1)} async-done(((bf16[8,128,384]{2,1,0:T(8,128)(2,1)}), bf16[16,128,384]{2,1,0:T(8,128)(2,1)}) %all-gather.9.cloned.1.call-update) | async-done | bytes 1572880 | tf_op jit(solution)/shard_map/all_gather | solution.py:54
  189.7 2.6 %gather_fusion.1 = bf16[32,128,384]{2,1,0:T(8,128)(2,1)S(1)} fusion(bf16[16,128,384]{2,1,0:T(8,128)(2,1)} %all-gather.9.cloned.1.call-done, s32[1024]{0:T(1024)S(1)} %pad_clamp_fusion), kind=kCustom, calls=%fused_computation.1 | custom fusion | bytes 6291584 | tf_op jit(solution)/shard_map/gather | solution.py:58
  192.4 2.6 %convert_reduce_fusion = f32[128,384]{1,0:T(8,128)} fusion(bf16[16,2,128,128]{3,2,1,0:T(8,128)(2,1)} %all-to-all-done.2, bf16[16,2,128,384]{3,2,1,0:T(8,128)(2,1)S(1)} %bitcast.56), kind=kOutput, calls=%fused_computation.6 | convolution fusion | flops 404963328 | bytes 4390912 | tf_op jit(solution)/shard_map/rsab,rsbh->rah/dot_general | solution.py:59
  195.0 1.0 reduce_sum.76
  196.0 1.4 fusion.12
  197.4 0.3 multiply_reduce_fusion
  197.7 0.2 add_convert_fusion
  197.9 0.1 copy.39
  198.0 15.5 %all_to_all.37 = bf16[8,8,2,384]{3,2,0,1:T(2,128)(2,1)S(1)} all-to-all(bf16[8,8,2,384]{3,2,0,1:T(2,128)(2,1)S(1)} %copy.39), channel_id=1, replica_groups=mesh['rx'=8,'rc'=2,'cz'=8,'cy'=8] {'cy'}, dimensions={1} | all-to-all | bytes 196608 | tf_op jit(solution)/shard_map/all_to_all | solution.py:22
  213.5 0.1 copy.40
  213.5 16.6 %all_to_all.38 = bf16[8,8,2,384]{3,2,1,0:T(2,128)(2,1)S(1)} all-to-all(bf16[8,8,2,384]{3,2,1,0:T(2,128)(2,1)S(1)} %copy.40), channel_id=1, replica_groups=mesh['rx'=8,'rc'=2,'cz'=8,'cy'=8] {'cz'}, dimensions={0} | all-to-all | bytes 196608 | tf_op jit(solution)/shard_map/all_to_all | solution.py:23
  230.2 0.7 reshape.321
  (8 shorter events, 0.1 us)
Async XLA Ops:
  6.5 65.0 %copy-start = (bf16[384,384]{1,0:T(8,128)(2,1)S(1)}, bf16[384,384]{1,0:T(8,128)(2,1)}, u32[]{:S(2)}) copy-start(bf16[384,384]{1,0:T(8,128)(2,1)} %param.9) | copy-start | bytes 884740
  8.2 16.3 %all-to-all-start = ((bf16[8,8,2,384]{3,2,0,1:T(2,128)(2,1)}), bf16[8,8,2,384]{3,2,0,1:T(2,128)(2,1)S(1)}, u32[]{:S(2)}, u32[]{:S(2)}) async-start(bf16[8,8,2,384]{3,2,0,1:T(2,128)(2,1)} %copy.34), calls=%async_computation | async-start | bytes 196608 | tf_op jit(solution)/shard_map/all_to_all | solution.py:22
  25.2 25.4 %all-to-all-start.1 = ((bf16[8,8,2,384]{3,2,1,0:T(2,128)(2,1)}), bf16[8,8,2,384]{3,2,1,0:T(2,128)(2,1)S(1)}, u32[]{:S(2)}, u32[]{:S(2)}) async-start(bf16[8,8,2,384]{3,2,1,0:T(2,128)(2,1)} %copy.35), calls=%async_computation.1 | async-start | bytes 196608 | tf_op jit(solution)/shard_map/all_to_all | solution.py:23
  50.6 13.8 %all-to-all-start.3 = ((s32[16,1,2]{2,1,0:T(1,128)}), s32[16,1,2]{2,1,0:T(1,128)S(1)}, u32[]{:S(2)}, u32[]{:S(2)}) async-start(s32[16,1,2]{2,1,0:T(1,128)} %bitcast.9), calls=%async_computation.3 | async-start | bytes 16384 | tf_op jit(solution)/shard_map/all_to_all | solution.py:77
  64.5 56.5 %copy-start.2 = (bf16[128,384]{1,0:T(8,128)(2,1)}, bf16[128,384]{1,0:T(8,128)(2,1)S(1)}, u32[]{:S(2)}) copy-start(bf16[128,384]{1,0:T(8,128)(2,1)S(1)} %reshape.318) | copy-start | bytes 294916
  64.5 68.7 %all-to-all-start.2 = ((bf16[16,2,128,128]{3,2,1,0:T(8,128)(2,1)}), bf16[16,2,128,128]{3,2,1,0:T(8,128)(2,1)}, u32[]{:S(2)}, u32[]{:S(2)}) async-start(bf16[16,2,128,128]{3,2,1,0:T(8,128)(2,1)} %bitcast.6), calls=%async_computation.2 | async-start | bytes 2097152 | tf_op jit(solution)/shard_map/all_to_all | solution.py:76
  71.5 59.1 %all-gather.7.cloned.1.call-start = ((), (), s32[]{:S(2)}) async-start(), calls=%async_computation.6 | async-start | bytes 2359296 | tf_op jit(solution)/shard_map/all_gather | solution.py:54
  120.6 69.1 %all-gather.9.cloned.1.call-start = ((), (), s32[]{:S(2)}) async-start(), calls=%async_computation.7 | async-start | bytes 2359296 | tf_op jit(solution)/shard_map/all_gather | solution.py:54
  133.2 4.5 %copy-start.5 = (f32[384]{0:T(512)S(1)}, f32[384]{0:T(512)}, u32[]{:S(2)}) copy-start(f32[384]{0:T(512)} %param.15) | copy-start | bytes 4612
  133.2 4.5 %copy-start.6 = (f32[384]{0:T(512)S(1)}, f32[384]{0:T(512)}, u32[]{:S(2)}) copy-start(f32[384]{0:T(512)} %param.14) | copy-start | bytes 4612
  136.9 30.3 %copy-start.1 = (f32[8,8,2,384]{3,2,1,0:T(2,128)}, f32[8,8,2,384]{3,2,1,0:T(2,128)S(1)}, u32[]{:S(2)}) copy-start(f32[8,8,2,384]{3,2,1,0:T(2,128)S(1)} %reduce_sum.72) | copy-start | bytes 589828
  137.1 30.1 %copy-start.3 = (f32[8,8,2]{2,1,0:T(8,128)}, f32[8,8,2]{2,1,0:T(8,128)S(1)}, u32[]{:S(2)}) copy-start(f32[8,8,2]{2,1,0:T(8,128)S(1)} %broadcast_multiply_fusion.1) | copy-start | bytes 1540
  137.6 29.7 %copy-start.4 = (f32[8,8,2]{2,1,0:T(8,128)}, f32[8,8,2]{2,1,0:T(8,128)S(1)}, u32[]{:S(2)}) copy-start(f32[8,8,2]{2,1,0:T(8,128)S(1)} %add_rsqrt_fusion.1) | copy-start | bytes 1540
Sparse Core Ops, SparseCore 0:
  120.7 9.7 all-gather.6
  167.3 22.3 all-gather.8

commit v3 on v1

--- a/solution.py
+++ b/solution.py
@@ -52,6 +52,16 @@
     return jnp.sum(per_source.astype(jnp.bfloat16).astype(jnp.float32), axis=0)
 
 
+def mix_and_couple(hidden, mix_weight, owned_blocks, owned_cols, chunks):
+    width = mix_weight.shape[1] // chunks
+    parts = []
+    for chunk in range(chunks):
+        weight = mix_weight[:, chunk * width:(chunk + 1) * width]
+        mixed = jnp.dot(hidden, weight, preferred_element_type=jnp.float32).astype(jnp.bfloat16)
+        parts.append(couple(mixed, owned_blocks, owned_cols))
+    return jnp.concatenate(parts, axis=-1)
+
+
 def body(states, mix_weight, coherence, block_row, block_col, block_count, gain, bias):
     blocks = coherence[0, 0]
     row_ids = block_row[0, 0]
@@ -63,12 +73,12 @@
     seat_blocks, seat_cols = seat_layout(
         blocks, row_ids, col_ids, live_count, row_groups, seats_per_row
     )
+    states, seat_blocks, seat_cols = lax.optimization_barrier((states, seat_blocks, seat_cols))
     owned_blocks = lax.all_to_all(seat_blocks, "row", split_axis=0, concat_axis=0, tiled=True)
     owned_cols = lax.all_to_all(seat_cols, "row", split_axis=0, concat_axis=0, tiled=True)
     hidden = to_grid(states)
     for iteration in range(ITERS):
-        mixed = jnp.dot(hidden, mix_weight, preferred_element_type=jnp.float32).astype(jnp.bfloat16)
-        coupled = couple(mixed, owned_blocks, owned_cols)
+        coupled = mix_and_couple(hidden, mix_weight, owned_blocks, owned_cols, 2)
         hidden = normalize(hidden, coupled, gain, bias)
     return to_grid(hidden)
 

time: 185 us -> 192 us (1.038)
  the two profiles are of different devices: /device:TPU:6 before, /device:TPU:2 now
where the time goes in v3:
time: 192 us; the launch traced here: 191 us
  blocking collectives  107 us (56%)
  starting transfers between devices  36.1 us (19%)
  waiting for transfers between devices  18 us (9%)
  local copies, waits for them, and re-layouts  16.8 us (9%)
  matrix products  9.25 us (5%)
  other arithmetic  3.31 us (2%)
    all_gather x4, blocking collectives, couple(): pieces_all = lax.all_gather(grid_mixed, 'row', axis=0, tiled=False)  90.2 us
    all_to_all x1, blocking collectives, to_grid(): lax.all_to_all(values, 'col', split_axis=0, concat_axis=0, tiled=True)  16.6 us
    all_to_all x1, starting transfers between devices, body(): lax.all_to_all(seat_cols, 'row', split_axis=0, concat_axis=0, tiled=True)  16.3 us
    all_to_all x1, starting transfers between devices, to_grid(): lax.all_to_all(values, 'col', split_axis=0, concat_axis=0, tiled=True)  14.2 us
    all_to_all x1, waiting for transfers between devices, to_grid(): lax.all_to_all(values, 'col', split_axis=0, concat_axis=0, tiled=True)  12.4 us
    dot_general x4, matrix products, couple(): jnp.einsum('rsab,rsbh->rah', owned_blocks, pieces, preferred_element_type...  8.04 us
    all_to_all x1, waiting for transfers between devices, body(): lax.all_to_all(seat_cols, 'row', split_axis=0, concat_axis=0, tiled=True)  5.59 us
    all_to_all x1, starting transfers between devices, body(): lax.all_to_all(seat_blocks, 'row', split_axis=0, concat_axis=0, tiled=True)  5.53 us
  transfers between devices with their start and end apart: 3, of which 2 were waited for; matrix products, arithmetic and copies ran while one was open for 2% of the time, Pallas kernels for 0%

profile of v3, /device:TPU:2, one launch (start us, length us, event | category | flops | bytes accessed | tf_op | source)
XLA Modules:
  0.0 191.3 jit_solution(14060852995859989437)
XLA Ops:
  0.8 0.9 convert_reduce_fusion.4
  1.7 0.7 fusion.11
  2.3 0.8 scatter_custom_fusion.1
  3.1 0.7 reshape.232
  3.8 1.2 broadcast_in_dim.6
  5.1 0.0 copy-done.2
  5.1 4.6 %scatter_fusion = bf16[32,128,128]{2,1,0:T(8,128)(2,1)} fusion(bf16[32,128,128]{2,1,0:T(8,128)(2,1)} %broadcast_in_dim.6, s32[32]{0:T(128)S(1)} %fusion.11, bf16[32,128,128]{2,1,0:T(8,128)(2,1)S(1)} %bitcast.86), kind=kCustom, calls=%fused_computation.4 | custom fusion | bytes 3145856 | tf_op jit(solution)/shard_map/scatter | solution.py:37
  9.6 16.3 %all-to-all-start.2 = ((s32[16,1,2]{2,1,0:T(1,128)}), s32[16,1,2]{2,1,0:T(1,128)S(1)}, u32[]{:S(2)}, u32[]{:S(2)}) async-start(s32[16,1,2]{2,1,0:T(1,128)} %bitcast.22), calls=%async_computation.2 | async-start | bytes 16384 | tf_op jit(solution)/shard_map/all_to_all | solution.py:78
  26.0 0.7 all_to_all.25
  26.6 5.6 %all-to-all-done.2 = s32[16,1,2]{2,1,0:T(1,128)S(1)} async-done(((s32[16,1,2]{2,1,0:T(1,128)}), s32[16,1,2]{2,1,0:T(1,128)S(1)}, u32[]{:S(2)}, u32[]{:S(2)}) %all-to-all-start.2) | async-done | bytes 160 | tf_op jit(solution)/shard_map/all_to_all | solution.py:78
  32.2 14.2 %all-to-all-start = ((bf16[64,2,384]{2,1,0:T(2,128)(2,1)}), bf16[64,2,384]{2,1,0:T(2,128)(2,1)S(1)}, u32[]{:S(2)}, u32[]{:S(2)}) async-start(bf16[64,2,384]{2,1,0:T(2,128)(2,1)} %all_to_all.25), calls=%async_computation | async-start | bytes 196608 | tf_op jit(solution)/shard_map/all_to_all | solution.py:18
  46.5 0.1 copy.49
  46.5 12.4 %all-to-all-done = bf16[64,2,384]{2,1,0:T(2,128)(2,1)S(1)} async-done(((bf16[64,2,384]{2,1,0:T(2,128)(2,1)}), bf16[64,2,384]{2,1,0:T(2,128)(2,1)S(1)}, u32[]{:S(2)}, u32[]{:S(2)}) %all-to-all-start) | async-done | bytes 98336 | tf_op jit(solution)/shard_map/all_to_all | solution.py:18
  58.9 5.5 %all-to-all-start.1 = ((bf16[16,2,128,128]{3,2,1,0:T(8,128)(2,1)}), bf16[16,2,128,128]{3,2,1,0:T(8,128)(2,1)}, u32[]{:S(2)}, u32[]{:S(2)}) async-start(bf16[16,2,128,128]{3,2,1,0:T(8,128)(2,1)} %bitcast.6), calls=%async_computation.1 | async-start | bytes 2097152 | tf_op jit(solution)/shard_map/all_to_all | solution.py:77
  64.4 0.1 copy.50
  64.5 0.1 reshape.235
  64.7 0.7 copy.55
  65.4 0.4 convolution_convert_fusion.2
  65.8 36.8 %all-gather.1 = bf16[2048,192]{0,1:T(8,128)(2,1)S(1)} all-gather(bf16[128,192]{0,1:T(8,128)(2,1)S(1)} %convolution_convert_fusion.2), channel_id=3, replica_groups=mesh['row'=16,'col'=64] {'row'}, dimensions={0}, use_global_device_ids=true | all-gather | bytes 835584 | tf_op jit(solution)/shard_map/all_gather | solution.py:47
  102.6 0.2 copy_bitcast_fusion.2
  102.8 0.9 gather_fusion.1
  103.6 0.2 convolution_convert_fusion.3
  103.9 17.9 %all-gather = bf16[2048,192]{0,1:T(8,128)(2,1)S(1)} all-gather(bf16[128,192]{0,1:T(8,128)(2,1)S(1)} %convolution_convert_fusion.3), channel_id=2, replica_groups=mesh['row'=16,'col'=64] {'row'}, dimensions={0}, use_global_device_ids=true | all-gather | bytes 835584 | tf_op jit(solution)/shard_map/all_gather | solution.py:47
  121.8 0.2 copy_bitcast_fusion.3
  122.0 1.9 gather_fusion
  123.9 0.0 all-to-all-done.1
  123.9 2.6 %convert_reduce_fusion.2 = f32[128,192]{0,1:T(8,128)} fusion(bf16[16,2,128,128]{3,2,1,0:T(8,128)(2,1)} %all-to-all-done.1, bf16[16,2,128,192]{2,3,1,0:T(8,128)(2,1)S(1)} %bitcast.82), kind=kOutput, calls=%fused_computation.12 | convolution fusion | flops 202481664 | bytes 2719744 | tf_op jit(solution)/shard_map/rsab,rsbh->rah/dot_general | solution.py:49
  126.5 1.0 copy.54
  127.5 0.1 concatenate.25
  127.6 0.0 copy-start.3
  127.6 0.0 copy-start.4
  127.6 0.0 copy-start.6
  127.6 0.0 copy-start.7
  127.6 1.9 convert_reduce_fusion.3
  129.5 0.1 copy.52
  129.6 0.1 concatenate.24
  129.7 0.3 fusion.15
  130.0 0.1 div.16
  130.2 0.2 multiply_reduce_fusion.1
  130.4 0.1 rsqrt.21
  130.6 0.0 copy-done.3
  130.6 0.0 copy-done.4
  130.6 0.0 copy-done.6
  130.6 0.0 copy-done.7
  130.6 0.2 fusion.4
  130.8 0.4 convolution_convert_fusion
  131.2 0.2 convolution_convert_fusion.1
  131.4 16.6 %all-gather.3 = bf16[2048,192]{0,1:T(8,128)(2,1)S(1)} all-gather(bf16[128,192]{0,1:T(8,128)(2,1)S(1)} %convolution_convert_fusion), channel_id=5, replica_groups=mesh['row'=16,'col'=64] {'row'}, dimensions={0}, use_global_device_ids=true | all-gather | bytes 835584 | tf_op jit(solution)/shard_map/all_gather | solution.py:47
  148.1 0.2 copy_bitcast_fusion
  148.3 0.9 gather_fusion.3
  149.1 1.8 convert_reduce_fusion
  150.9 0.1 copy.59
  151.0 0.1 concatenate.29
  151.1 18.8 %all-gather.2 = bf16[2048,192]{0,1:T(8,128)(2,1)S(1)} all-gather(bf16[128,192]{0,1:T(8,128)(2,1)S(1)} %convolution_convert_fusion.1), channel_id=4, replica_groups=mesh['row'=16,'col'=64] {'row'}, dimensions={0}, use_global_device_ids=true | all-gather | bytes 835584 | tf_op jit(solution)/shard_map/all_gather | solution.py:47
  169.9 0.2 copy_bitcast_fusion.1
  170.1 0.9 gather_fusion.2
  171.0 1.8 convert_reduce_fusion.1
  172.8 0.1 copy.57
  172.9 0.1 concatenate.28
  173.0 0.5 fusion.14
  173.5 0.2 multiply_reduce_fusion
  173.7 0.2 add_convert_fusion
  174.0 16.6 %all_to_all.38 = bf16[64,2,384]{2,1,0:T(2,128)(2,1)S(1)} all-to-all(bf16[64,2,384]{2,1,0:T(2,128)(2,1)S(1)} %add_convert_fusion), channel_id=1, replica_groups=mesh['row'=16,'col'=64] {'col'}, dimensions={0} | all-to-all | bytes 196608 | tf_op jit(solution)/shard_map/all_to_all | solution.py:18
  190.6 0.7 all_to_all.33
  (15 shorter events, 0.1 us)
Async XLA Ops:
  0.0 5.1 %copy-start.2 = (bf16[1,1,32,128,128]{4,3,2,1,0:T(8,128)(2,1)S(1)}, bf16[1,1,32,128,128]{4,3,2,1,0:T(8,128)(2,1)}, u32[]{:S(2)}) copy-start(bf16[1,1,32,128,128]{4,3,2,1,0:T(8,128)(2,1)} %param.10) | copy-start | bytes 3145732
  5.1 20.9 %copy-start.5 = (bf16[128,384]{1,0:T(8,128)(2,1)S(1)}, bf16[128,384]{1,0:T(8,128)(2,1)}, u32[]{:S(2)}) copy-start(bf16[128,384]{1,0:T(8,128)(2,1)} %param.8) | copy-start | bytes 294916
  9.6 55.8 %copy-start.1 = (bf16[384,384]{1,0:T(8,128)(2,1)S(1)}, bf16[384,384]{1,0:T(8,128)(2,1)}, u32[]{:S(2)}) copy-start(bf16[384,384]{1,0:T(8,128)(2,1)} %param.9) | copy-start | bytes 884740
  9.6 22.6 %all-to-all-start.2 = ((s32[16,1,2]{2,1,0:T(1,128)}), s32[16,1,2]{2,1,0:T(1,128)S(1)}, u32[]{:S(2)}, u32[]{:S(2)}) async-start(s32[16,1,2]{2,1,0:T(1,128)} %bitcast.22), calls=%async_computation.2 | async-start | bytes 16384 | tf_op jit(solution)/shard_map/all_to_all | solution.py:78
  32.2 26.7 %all-to-all-start = ((bf16[64,2,384]{2,1,0:T(2,128)(2,1)}), bf16[64,2,384]{2,1,0:T(2,128)(2,1)S(1)}, u32[]{:S(2)}, u32[]{:S(2)}) async-start(bf16[64,2,384]{2,1,0:T(2,128)(2,1)} %all_to_all.25), calls=%async_computation | async-start | bytes 196608 | tf_op jit(solution)/shard_map/all_to_all | solution.py:18
  58.9 65.0 %all-to-all-start.1 = ((bf16[16,2,128,128]{3,2,1,0:T(8,128)(2,1)}), bf16[16,2,128,128]{3,2,1,0:T(8,128)(2,1)}, u32[]{:S(2)}, u32[]{:S(2)}) async-start(bf16[16,2,128,128]{3,2,1,0:T(8,128)(2,1)} %bitcast.6), calls=%async_computation.1 | async-start | bytes 2097152 | tf_op jit(solution)/shard_map/all_to_all | solution.py:77
  123.9 3.6 %copy-start = (bf16[32,128,192]{1,2,0:T(8,128)(2,1)S(1)}, bf16[32,128,192]{1,2,0:T(8,128)(2,1)}, u32[]{:S(2)}) copy-start(bf16[32,128,192]{1,2,0:T(8,128)(2,1)} %gather_fusion) | copy-start | bytes 4718596
  127.6 3.0 %copy-start.3 = (f32[128,192]{0,1:T(8,128)S(1)}, f32[128,192]{0,1:T(8,128)}, u32[]{:S(2)}) copy-start(f32[128,192]{0,1:T(8,128)} %convert_reduce_fusion.2) | copy-start | bytes 294916
  127.6 3.0 %copy-start.4 = (bf16[128,384]{0,1:T(8,128)(2,1)S(1)}, bf16[128,384]{0,1:T(8,128)(2,1)}, u32[]{:S(2)}) copy-start(bf16[128,384]{0,1:T(8,128)(2,1)} %copy.55) | copy-start | bytes 294916
  127.6 3.0 %copy-start.6 = (f32[384]{0:T(512)S(1)}, f32[384]{0:T(512)}, u32[]{:S(2)}) copy-start(f32[384]{0:T(512)} %param.15) | copy-start | bytes 4612
  127.6 3.0 %copy-start.7 = (f32[384]{0:T(512)S(1)}, f32[384]{0:T(512)}, u32[]{:S(2)}) copy-start(f32[384]{0:T(512)} %param.14) | copy-start | bytes 4612

commit v4 on v3

--- a/solution.py
+++ b/solution.py
@@ -2,6 +2,7 @@
 import jax.numpy as jnp
 from jax import lax
 from jax.sharding import PartitionSpec as P
+
 
 ITERS = 2
 
@@ -16,6 +17,16 @@
 
 def to_grid(values):
     return lax.all_to_all(values, "col", split_axis=0, concat_axis=0, tiled=True)
+
+
+def send_rows(bundle, row_groups):
+    me = lax.axis_index("row")
+    received = [lax.dynamic_index_in_dim(bundle, me, 0, keepdims=False)]
+    for shift in range(1, row_groups):
+        outgoing = lax.dynamic_index_in_dim(bundle, (me + shift) % row_groups, 0, keepdims=False)
+        pairs = [(source, (source + shift) % row_groups) for source in range(row_groups)]
+        received.append(lax.ppermute(outgoing, "row", pairs))
+    return jnp.stack(received)
 
 
 def seat_layout(blocks, row_ids, col_ids, live_count, row_groups, seats_per_row):
@@ -62,7 +73,7 @@
     return jnp.concatenate(parts, axis=-1)
 
 
-def body(states, mix_weight, coherence, block_row, block_col, block_count, gain, bias):
+def layer(states, mix_weight, coherence, block_row, block_col, block_count, gain, bias):
     blocks = coherence[0, 0]
     row_ids = block_row[0, 0]
     col_ids = block_col[0, 0]
@@ -74,10 +85,21 @@
         blocks, row_ids, col_ids, live_count, row_groups, seats_per_row
     )
     states, seat_blocks, seat_cols = lax.optimization_barrier((states, seat_blocks, seat_cols))
-    owned_blocks = lax.all_to_all(seat_blocks, "row", split_axis=0, concat_axis=0, tiled=True)
-    owned_cols = lax.all_to_all(seat_cols, "row", split_axis=0, concat_axis=0, tiled=True)
+    block_len = blocks.shape[-1]
+    tail = 16
+    col_rows = jnp.broadcast_to(
+        seat_cols.astype(blocks.dtype)[:, :, None], (row_groups, seats_per_row, block_len)
+    )
+    col_rows = jnp.pad(col_rows, ((0, 0), (0, tail - seats_per_row), (0, 0)))
+    bundle = jnp.concatenate(
+        [seat_blocks.reshape(row_groups, seats_per_row * block_len, block_len), col_rows], axis=1
+    )
+    bundle = send_rows(bundle, row_groups)
+    owned_blocks = bundle[:, : seats_per_row * block_len].reshape(seat_blocks.shape)
+    owned_cols = bundle[:, seats_per_row * block_len : seats_per_row * block_len + seats_per_row, 0]
+    owned_cols = owned_cols.astype(jnp.int32)
     hidden = to_grid(states)
-    for iteration in range(ITERS):
+    for _ in range(ITERS):
         coupled = mix_and_couple(hidden, mix_weight, owned_blocks, owned_cols, 2)
         hidden = normalize(hidden, coupled, gain, bias)
     return to_grid(hidden)
@@ -95,5 +117,5 @@
         P(),
     )
     return jax.shard_map(
-        body, mesh=mesh, in_specs=placed, out_specs=P(("row", "col"), None), check_vma=False
+        layer, mesh=mesh, in_specs=placed, out_specs=P(("row", "col"), None), check_vma=False
     )

time: 192 us -> 210 us (1.094)
  starting transfers between devices: 36.1 us -> 75.5 us
  waiting for transfers between devices: 18 us -> 0.04 us
  blocking collectives: 107 us -> 95.9 us
  local copies, waits for them, and re-layouts: 16.8 us -> 24.1 us
    ppermute x0 -> x15, starting transfers between devices: none -> 64.5 us  [send_rows(): received.append(lax.ppermute(outgoing, 'row', pairs))]
    all_to_all x2 -> x0, starting transfers between devices: 21.9 us -> none  [the longest x1 16.3 us: body(): lax.all_to_all(seat_cols, 'row', split_axis=0, concat_axis=0, tiled=True)]
    all_gather x4, blocking collectives: 90.2 us -> 70.8 us  [couple(): pieces_all = lax.all_gather(grid_mixed, 'row', axis=0, tiled=False)]
    all_to_all x1, waiting for transfers between devices: 12.4 us -> 0.01 us  [to_grid(): lax.all_to_all(values, 'col', split_axis=0, concat_axis=0, tiled=True)]
    unnamed x16 -> x30, local copies, waits for them, and re-layouts: 0.04 us -> 8.93 us
    all_to_all x1, blocking collectives: 16.6 us -> 25 us  [to_grid(): lax.all_to_all(values, 'col', split_axis=0, concat_axis=0, tiled=True)]
    all_to_all x2 -> x0, waiting for transfers between devices: 5.59 us -> none  [the longest x1 5.59 us: body(): lax.all_to_all(seat_cols, 'row', split_axis=0, concat_axis=0, tiled=True)]
    all_to_all x1, starting transfers between devices: 14.2 us -> 11 us  [to_grid(): lax.all_to_all(values, 'col', split_axis=0, concat_axis=0, tiled=True)]
  transfers between devices with their start and end apart: 3 -> 16, of which waited for: 2 -> 0; matrix products, arithmetic and copies ran while one was open for 2% -> 6% of each run, Pallas kernels for 0% -> 0%
where the time goes in v4:
time: 210 us; the launch traced here: 209 us
  blocking collectives  95.9 us (46%)
  starting transfers between devices  75.5 us (36%)
  local copies, waits for them, and re-layouts  24.1 us (11%)
  matrix products  7.33 us (3%)
  other arithmetic  4.5 us (2%)
    all_gather x4, blocking collectives, couple(): pieces_all = lax.all_gather(grid_mixed, 'row', axis=0, tiled=False)  70.8 us
    ppermute x15, starting transfers between devices, send_rows(): received.append(lax.ppermute(outgoing, 'row', pairs))  64.5 us
    all_to_all x1, blocking collectives, to_grid(): lax.all_to_all(values, 'col', split_axis=0, concat_axis=0, tiled=True)  25 us
    all_to_all x1, starting transfers between devices, to_grid(): lax.all_to_all(values, 'col', split_axis=0, concat_axis=0, tiled=True)  11 us
    unnamed x30, local copies, waits for them, and re-layouts  8.93 us
    dot_general x4, matrix products, couple(): jnp.einsum('rsab,rsbh->rah', owned_blocks, pieces, preferred_element_type...  6.12 us
    gather x4, local copies, waits for them, and re-layouts, couple(): pieces = pieces_all[owned_cols]  4.46 us
  transfers between devices with their start and end apart: 16, of which 0 were waited for; matrix products, arithmetic and copies ran while one was open for 6% of the time, Pallas kernels for 0%

profile of v4, /device:TPU:2, one launch (start us, length us, event | category | flops | bytes accessed | tf_op | source)
XLA Modules:
  0.0 208.7 jit_solution(1909238479353852191)
XLA Ops:
  0.8 0.9 convert_reduce_fusion.4
  1.7 0.7 fusion.14
  2.3 0.8 scatter_custom_fusion.1
  3.2 0.2 broadcast_in_dim.8
  3.5 1.7 scatter_fusion
  5.5 0.9 dynamic-slice_bitcast_fusion
  6.4 3.4 %collective-permute-start.1 = (bf16[272,128]{1,0:T(8,128)(2,1)S(1)}, bf16[272,128]{1,0:T(8,128)(2,1)S(1)}, u32[]{:S(2)}, u32[]{:S(2)}) collective-permute-start(bf16[272,128]{1,0:T(8,128)(2,1)S(1)} %get-tuple-element.28), channel_id=1, source_target_pairs={{0,128},{64,192},{128,256},{192,320},{256,384},{320,448},{384,512}... | collective-permute-start | bytes 208904 | tf_op jit(solution)/shard_map/ppermute | solution.py:28
  9.8 5.6 %collective-permute-start.2 = (bf16[272,128]{1,0:T(8,128)(2,1)S(1)}, bf16[272,128]{1,0:T(8,128)(2,1)S(1)}, u32[]{:S(2)}, u32[]{:S(2)}) collective-permute-start(bf16[272,128]{1,0:T(8,128)(2,1)S(1)} %get-tuple-element.27), channel_id=1, source_target_pairs={{0,192},{64,256},{128,320},{192,384},{256,448},{320,512},{384,576}... | collective-permute-start | bytes 208904 | tf_op jit(solution)/shard_map/ppermute | solution.py:28
  15.3 2.5 %collective-permute-start.3 = (bf16[272,128]{1,0:T(8,128)(2,1)S(1)}, bf16[272,128]{1,0:T(8,128)(2,1)S(1)}, u32[]{:S(2)}, u32[]{:S(2)}) collective-permute-start(bf16[272,128]{1,0:T(8,128)(2,1)S(1)} %get-tuple-element.26), channel_id=1, source_target_pairs={{0,256},{64,320},{128,384},{192,448},{256,512},{320,576},{384,640}... | collective-permute-start | bytes 208904 | tf_op jit(solution)/shard_map/ppermute | solution.py:28
  17.9 14.4 %collective-permute-start.4 = (bf16[272,128]{1,0:T(8,128)(2,1)S(1)}, bf16[272,128]{1,0:T(8,128)(2,1)S(1)}, u32[]{:S(2)}, u32[]{:S(2)}) collective-permute-start(bf16[272,128]{1,0:T(8,128)(2,1)S(1)} %get-tuple-element.25), channel_id=1, source_target_pairs={{0,320},{64,384},{128,448},{192,512},{256,576},{320,640},{384,704}... | collective-permute-start | bytes 208904 | tf_op jit(solution)/shard_map/ppermute | solution.py:28
  32.3 0.7 all_to_all.14
  33.0 11.0 %all-to-all-start = ((bf16[64,2,384]{2,1,0:T(2,128)(2,1)}), bf16[64,2,384]{2,1,0:T(2,128)(2,1)S(1)}, u32[]{:S(2)}, u32[]{:S(2)}) async-start(bf16[64,2,384]{2,1,0:T(2,128)(2,1)} %all_to_all.14), calls=%async_computation | async-start | bytes 196608 | tf_op jit(solution)/shard_map/all_to_all | solution.py:19
  43.9 5.1 %collective-permute-start.5 = (bf16[272,128]{1,0:T(8,128)(2,1)S(1)}, bf16[272,128]{1,0:T(8,128)(2,1)S(1)}, u32[]{:S(2)}, u32[]{:S(2)}) collective-permute-start(bf16[272,128]{1,0:T(8,128)(2,1)S(1)} %get-tuple-element.24), channel_id=1, source_target_pairs={{0,384},{64,448},{128,512},{192,576},{256,640},{320,704},{384,768}... | collective-permute-start | bytes 208904 | tf_op jit(solution)/shard_map/ppermute | solution.py:28
  49.0 0.6 bitcast_dynamic-update-slice_fusion.14
  49.7 4.4 %collective-permute-start.6 = (bf16[272,128]{1,0:T(8,128)(2,1)S(1)}, bf16[272,128]{1,0:T(8,128)(2,1)S(1)}, u32[]{:S(2)}, u32[]{:S(2)}) collective-permute-start(bf16[272,128]{1,0:T(8,128)(2,1)S(1)} %get-tuple-element.23), channel_id=1, source_target_pairs={{0,448},{64,512},{128,576},{192,640},{256,704},{320,768},{384,832}... | collective-permute-start | bytes 208904 | tf_op jit(solution)/shard_map/ppermute | solution.py:28
  54.1 0.6 bitcast_dynamic-update-slice_fusion.13
  54.7 5.1 %collective-permute-start.7 = (bf16[272,128]{1,0:T(8,128)(2,1)S(1)}, bf16[272,128]{1,0:T(8,128)(2,1)S(1)}, u32[]{:S(2)}, u32[]{:S(2)}) collective-permute-start(bf16[272,128]{1,0:T(8,128)(2,1)S(1)} %get-tuple-element.22), channel_id=1, source_target_pairs={{0,512},{64,576},{128,640},{192,704},{256,768},{320,832},{384,896}... | collective-permute-start | bytes 208904 | tf_op jit(solution)/shard_map/ppermute | solution.py:28
  59.8 0.6 bitcast_dynamic-update-slice_fusion.12
  60.4 4.4 %collective-permute-start.8 = (bf16[272,128]{1,0:T(8,128)(2,1)S(1)}, bf16[272,128]{1,0:T(8,128)(2,1)S(1)}, u32[]{:S(2)}, u32[]{:S(2)}) collective-permute-start(bf16[272,128]{1,0:T(8,128)(2,1)S(1)} %get-tuple-element.21), channel_id=1, source_target_pairs={{0,576},{64,640},{128,704},{192,768},{256,832},{320,896},{384,960}... | collective-permute-start | bytes 208904 | tf_op jit(solution)/shard_map/ppermute | solution.py:28
  64.8 0.6 bitcast_dynamic-update-slice_fusion.11
  65.4 6.3 %collective-permute-start.9 = (bf16[272,128]{1,0:T(8,128)(2,1)S(1)}, bf16[272,128]{1,0:T(8,128)(2,1)S(1)}, u32[]{:S(2)}, u32[]{:S(2)}) collective-permute-start(bf16[272,128]{1,0:T(8,128)(2,1)S(1)} %get-tuple-element.20), channel_id=1, source_target_pairs={{0,640},{64,704},{128,768},{192,832},{256,896},{320,960},{384,0},{... | collective-permute-start | bytes 208904 | tf_op jit(solution)/shard_map/ppermute | solution.py:28
  71.8 0.6 bitcast_dynamic-update-slice_fusion.10
  72.4 1.9 collective-permute-start.10
  74.3 0.6 bitcast_dynamic-update-slice_fusion.9
  74.9 2.6 %collective-permute-start.11 = (bf16[272,128]{1,0:T(8,128)(2,1)S(1)}, bf16[272,128]{1,0:T(8,128)(2,1)S(1)}, u32[]{:S(2)}, u32[]{:S(2)}) collective-permute-start(bf16[272,128]{1,0:T(8,128)(2,1)S(1)} %get-tuple-element.18), channel_id=1, source_target_pairs={{0,768},{64,832},{128,896},{192,960},{256,0},{320,64},{384,128},{4... | collective-permute-start | bytes 208904 | tf_op jit(solution)/shard_map/ppermute | solution.py:28
  77.5 0.6 bitcast_dynamic-update-slice_fusion.8
  78.1 4.2 %collective-permute-start.12 = (bf16[272,128]{1,0:T(8,128)(2,1)S(1)}, bf16[272,128]{1,0:T(8,128)(2,1)S(1)}, u32[]{:S(2)}, u32[]{:S(2)}) collective-permute-start(bf16[272,128]{1,0:T(8,128)(2,1)S(1)} %get-tuple-element.17), channel_id=1, source_target_pairs={{0,832},{64,896},{128,960},{192,0},{256,64},{320,128},{384,192},{4... | collective-permute-start | bytes 208904 | tf_op jit(solution)/shard_map/ppermute | solution.py:28
  82.3 0.6 bitcast_dynamic-update-slice_fusion.7
  83.0 4.5 %collective-permute-start.13 = (bf16[272,128]{1,0:T(8,128)(2,1)S(1)}, bf16[272,128]{1,0:T(8,128)(2,1)S(1)}, u32[]{:S(2)}, u32[]{:S(2)}) collective-permute-start(bf16[272,128]{1,0:T(8,128)(2,1)S(1)} %get-tuple-element.16), channel_id=1, source_target_pairs={{0,896},{64,960},{128,0},{192,64},{256,128},{320,192},{384,256},{4... | collective-permute-start | bytes 208904 | tf_op jit(solution)/shard_map/ppermute | solution.py:28
  87.5 0.6 bitcast_dynamic-update-slice_fusion.6
  88.1 0.3 collective-permute-start.14
  88.4 0.6 bitcast_dynamic-update-slice_fusion.5
  89.0 0.6 bitcast_dynamic-update-slice_fusion.4
  89.7 0.6 bitcast_dynamic-update-slice_fusion.3
  90.3 0.6 bitcast_dynamic-update-slice_fusion.2
  90.9 0.7 bitcast_dynamic-update-slice_fusion.1
  91.6 0.6 bitcast_dynamic-update-slice_fusion
  92.2 2.3 %slice.26 = bf16[16,256,128]{2,1,0:T(8,128)(2,1)} slice(bf16[16,272,128]{2,1,0:T(8,128)(2,1)} %bitcast_dynamic-update-slice_fusion), slice={[0:16], [0:256], [0:128]} | slice | bytes 2097152 | tf_op jit(solution)/shard_map/slice | solution.py:98
  94.6 1.1 fusion.11
  95.8 0.4 convolution_convert_fusion.2
  96.2 0.2 convolution_convert_fusion.3
  96.4 0.8 copy.40
  97.2 17.7 %all-gather.1 = bf16[2048,192]{0,1:T(8,128)(2,1)S(1)} all-gather(bf16[128,192]{0,1:T(8,128)(2,1)S(1)} %convolution_convert_fusion.2), channel_id=3, replica_groups=mesh['row'=16,'col'=64] {'row'}, dimensions={0}, use_global_device_ids=true | all-gather | bytes 835584 | tf_op jit(solution)/shard_map/all_gather | solution.py:58
  114.9 0.2 copy_bitcast_fusion.2
  115.1 18.3 %all-gather = bf16[2048,192]{0,1:T(8,128)(2,1)S(1)} all-gather(bf16[128,192]{0,1:T(8,128)(2,1)S(1)} %convolution_convert_fusion.3), channel_id=2, replica_groups=mesh['row'=16,'col'=64] {'row'}, dimensions={0}, use_global_device_ids=true | all-gather | bytes 835584 | tf_op jit(solution)/shard_map/all_gather | solution.py:58
  133.6 0.9 gather_fusion.1
  134.5 1.9 gather_fusion
  136.4 1.9 convert_reduce_fusion.2
  138.4 0.6 convert_reduce_fusion.3
  139.4 0.3 fusion.18
  139.9 0.2 multiply_reduce_fusion.1
  140.5 0.4 convolution_convert_fusion
  140.9 0.2 convolution_convert_fusion.1
  141.1 16.6 %all-gather.3 = bf16[2048,192]{0,1:T(8,128)(2,1)S(1)} all-gather(bf16[128,192]{0,1:T(8,128)(2,1)S(1)} %convolution_convert_fusion), channel_id=5, replica_groups=mesh['row'=16,'col'=64] {'row'}, dimensions={0}, use_global_device_ids=true | all-gather | bytes 835584 | tf_op jit(solution)/shard_map/all_gather | solution.py:58
  158.0 0.9 gather_fusion.3
  158.8 1.8 convert_reduce_fusion
  160.8 18.1 %all-gather.2 = bf16[2048,192]{0,1:T(8,128)(2,1)S(1)} all-gather(bf16[128,192]{0,1:T(8,128)(2,1)S(1)} %convolution_convert_fusion.1), channel_id=4, replica_groups=mesh['row'=16,'col'=64] {'row'}, dimensions={0}, use_global_device_ids=true | all-gather | bytes 835584 | tf_op jit(solution)/shard_map/all_gather | solution.py:58
  179.1 0.9 gather_fusion.2
  180.0 1.8 convert_reduce_fusion.1
  182.0 0.5 fusion.17
  182.5 0.2 multiply_reduce_fusion
  182.8 0.2 add_convert_fusion
  183.0 25.0 %all_to_all.21 = bf16[64,2,384]{2,1,0:T(2,128)(2,1)S(1)} all-to-all(bf16[64,2,384]{2,1,0:T(2,128)(2,1)S(1)} %add_convert_fusion), channel_id=1, replica_groups=mesh['row'=16,'col'=64] {'col'}, dimensions={0} | all-to-all | bytes 196608 | tf_op jit(solution)/shard_map/all_to_all | solution.py:19
  208.0 0.7 all_to_all.18
  (59 shorter events, 2.3 us)
Async XLA Ops:
  0.0 3.5 %copy-start.2 = (bf16[1,1,32,128,128]{4,3,2,1,0:T(8,128)(2,1)S(1)}, bf16[1,1,32,128,128]{4,3,2,1,0:T(8,128)(2,1)}, u32[]{:S(2)}) copy-start(bf16[1,1,32,128,128]{4,3,2,1,0:T(8,128)(2,1)} %param.10) | copy-start | bytes 3145732
  5.5 26.8 %copy-start.5 = (bf16[128,384]{1,0:T(8,128)(2,1)S(1)}, bf16[128,384]{1,0:T(8,128)(2,1)}, u32[]{:S(2)}) copy-start(bf16[128,384]{1,0:T(8,128)(2,1)} %param.8) | copy-start | bytes 294916
  6.4 37.5 %collective-permute-start = (bf16[272,128]{1,0:T(8,128)(2,1)S(1)}, bf16[272,128]{1,0:T(8,128)(2,1)S(1)}, u32[]{:S(2)}, u32[]{:S(2)}) collective-permute-start(bf16[272,128]{1,0:T(8,128)(2,1)S(1)} %get-tuple-element.29), channel_id=1, source_target_pairs={{0,64},{64,128},{128,192},{192,256},{256,320},{320,384},{384,448},... | collective-permute-start | bytes 208904 | tf_op jit(solution)/shard_map/ppermute | solution.py:28
  6.4 43.3 %collective-permute-start.1 = (bf16[272,128]{1,0:T(8,128)(2,1)S(1)}, bf16[272,128]{1,0:T(8,128)(2,1)S(1)}, u32[]{:S(2)}, u32[]{:S(2)}) collective-permute-start(bf16[272,128]{1,0:T(8,128)(2,1)S(1)} %get-tuple-element.28), channel_id=1, source_target_pairs={{0,128},{64,192},{128,256},{192,320},{256,384},{320,448},{384,512}... | collective-permute-start | bytes 208904 | tf_op jit(solution)/shard_map/ppermute | solution.py:28
  9.8 44.9 %collective-permute-start.2 = (bf16[272,128]{1,0:T(8,128)(2,1)S(1)}, bf16[272,128]{1,0:T(8,128)(2,1)S(1)}, u32[]{:S(2)}, u32[]{:S(2)}) collective-permute-start(bf16[272,128]{1,0:T(8,128)(2,1)S(1)} %get-tuple-element.27), channel_id=1, source_target_pairs={{0,192},{64,256},{128,320},{192,384},{256,448},{320,512},{384,576}... | collective-permute-start | bytes 208904 | tf_op jit(solution)/shard_map/ppermute | solution.py:28
  15.3 45.0 %collective-permute-start.3 = (bf16[272,128]{1,0:T(8,128)(2,1)S(1)}, bf16[272,128]{1,0:T(8,128)(2,1)S(1)}, u32[]{:S(2)}, u32[]{:S(2)}) collective-permute-start(bf16[272,128]{1,0:T(8,128)(2,1)S(1)} %get-tuple-element.26), channel_id=1, source_target_pairs={{0,256},{64,320},{128,384},{192,448},{256,512},{320,576},{384,640}... | collective-permute-start | bytes 208904 | tf_op jit(solution)/shard_map/ppermute | solution.py:28
  17.9 47.6 %collective-permute-start.4 = (bf16[272,128]{1,0:T(8,128)(2,1)S(1)}, bf16[272,128]{1,0:T(8,128)(2,1)S(1)}, u32[]{:S(2)}, u32[]{:S(2)}) collective-permute-start(bf16[272,128]{1,0:T(8,128)(2,1)S(1)} %get-tuple-element.25), channel_id=1, source_target_pairs={{0,320},{64,384},{128,448},{192,512},{256,576},{320,640},{384,704}... | collective-permute-start | bytes 208904 | tf_op jit(solution)/shard_map/ppermute | solution.py:28
  33.0 62.8 %all-to-all-start = ((bf16[64,2,384]{2,1,0:T(2,128)(2,1)}), bf16[64,2,384]{2,1,0:T(2,128)(2,1)S(1)}, u32[]{:S(2)}, u32[]{:S(2)}) async-start(bf16[64,2,384]{2,1,0:T(2,128)(2,1)} %all_to_all.14), calls=%async_computation | async-start | bytes 196608 | tf_op jit(solution)/shard_map/all_to_all | solution.py:19
  43.9 28.4 %collective-permute-start.5 = (bf16[272,128]{1,0:T(8,128)(2,1)S(1)}, bf16[272,128]{1,0:T(8,128)(2,1)S(1)}, u32[]{:S(2)}, u32[]{:S(2)}) collective-permute-start(bf16[272,128]{1,0:T(8,128)(2,1)S(1)} %get-tuple-element.24), channel_id=1, source_target_pairs={{0,384},{64,448},{128,512},{192,576},{256,640},{320,704},{384,768}... | collective-permute-start | bytes 208904 | tf_op jit(solution)/shard_map/ppermute | solution.py:28
  49.7 25.3 %collective-permute-start.6 = (bf16[272,128]{1,0:T(8,128)(2,1)S(1)}, bf16[272,128]{1,0:T(8,128)(2,1)S(1)}, u32[]{:S(2)}, u32[]{:S(2)}) collective-permute-start(bf16[272,128]{1,0:T(8,128)(2,1)S(1)} %get-tuple-element.23), channel_id=1, source_target_pairs={{0,448},{64,512},{128,576},{192,640},{256,704},{320,768},{384,832}... | collective-permute-start | bytes 208904 | tf_op jit(solution)/shard_map/ppermute | solution.py:28
  54.7 23.4 %collective-permute-start.7 = (bf16[272,128]{1,0:T(8,128)(2,1)S(1)}, bf16[272,128]{1,0:T(8,128)(2,1)S(1)}, u32[]{:S(2)}, u32[]{:S(2)}) collective-permute-start(bf16[272,128]{1,0:T(8,128)(2,1)S(1)} %get-tuple-element.22), channel_id=1, source_target_pairs={{0,512},{64,576},{128,640},{192,704},{256,768},{320,832},{384,896}... | collective-permute-start | bytes 208904 | tf_op jit(solution)/shard_map/ppermute | solution.py:28
  60.4 22.6 %collective-permute-start.8 = (bf16[272,128]{1,0:T(8,128)(2,1)S(1)}, bf16[272,128]{1,0:T(8,128)(2,1)S(1)}, u32[]{:S(2)}, u32[]{:S(2)}) collective-permute-start(bf16[272,128]{1,0:T(8,128)(2,1)S(1)} %get-tuple-element.21), channel_id=1, source_target_pairs={{0,576},{64,640},{128,704},{192,768},{256,832},{320,896},{384,960}... | collective-permute-start | bytes 208904 | tf_op jit(solution)/shard_map/ppermute | solution.py:28
  65.4 22.7 %collective-permute-start.9 = (bf16[272,128]{1,0:T(8,128)(2,1)S(1)}, bf16[272,128]{1,0:T(8,128)(2,1)S(1)}, u32[]{:S(2)}, u32[]{:S(2)}) collective-permute-start(bf16[272,128]{1,0:T(8,128)(2,1)S(1)} %get-tuple-element.20), channel_id=1, source_target_pairs={{0,640},{64,704},{128,768},{192,832},{256,896},{320,960},{384,0},{... | collective-permute-start | bytes 208904 | tf_op jit(solution)/shard_map/ppermute | solution.py:28
  72.4 16.7 %collective-permute-start.10 = (bf16[272,128]{1,0:T(8,128)(2,1)S(1)}, bf16[272,128]{1,0:T(8,128)(2,1)S(1)}, u32[]{:S(2)}, u32[]{:S(2)}) collective-permute-start(bf16[272,128]{1,0:T(8,128)(2,1)S(1)} %get-tuple-element.19), channel_id=1, source_target_pairs={{0,704},{64,768},{128,832},{192,896},{256,960},{320,0},{384,64},{4... | collective-permute-start | bytes 208904 | tf_op jit(solution)/shard_map/ppermute | solution.py:28
  74.9 14.7 %collective-permute-start.11 = (bf16[272,128]{1,0:T(8,128)(2,1)S(1)}, bf16[272,128]{1,0:T(8,128)(2,1)S(1)}, u32[]{:S(2)}, u32[]{:S(2)}) collective-permute-start(bf16[272,128]{1,0:T(8,128)(2,1)S(1)} %get-tuple-element.18), channel_id=1, source_target_pairs={{0,768},{64,832},{128,896},{192,960},{256,0},{320,64},{384,128},{4... | collective-permute-start | bytes 208904 | tf_op jit(solution)/shard_map/ppermute | solution.py:28
  78.1 12.2 %collective-permute-start.12 = (bf16[272,128]{1,0:T(8,128)(2,1)S(1)}, bf16[272,128]{1,0:T(8,128)(2,1)S(1)}, u32[]{:S(2)}, u32[]{:S(2)}) collective-permute-start(bf16[272,128]{1,0:T(8,128)(2,1)S(1)} %get-tuple-element.17), channel_id=1, source_target_pairs={{0,832},{64,896},{128,960},{192,0},{256,64},{320,128},{384,192},{4... | collective-permute-start | bytes 208904 | tf_op jit(solution)/shard_map/ppermute | solution.py:28
  83.0 8.0 %collective-permute-start.13 = (bf16[272,128]{1,0:T(8,128)(2,1)S(1)}, bf16[272,128]{1,0:T(8,128)(2,1)S(1)}, u32[]{:S(2)}, u32[]{:S(2)}) collective-permute-start(bf16[272,128]{1,0:T(8,128)(2,1)S(1)} %get-tuple-element.16), channel_id=1, source_target_pairs={{0,896},{64,960},{128,0},{192,64},{256,128},{320,192},{384,256},{4... | collective-permute-start | bytes 208904 | tf_op jit(solution)/shard_map/ppermute | solution.py:28
  88.1 3.5 %collective-permute-start.14 = (bf16[272,128]{1,0:T(8,128)(2,1)S(1)}, bf16[272,128]{1,0:T(8,128)(2,1)S(1)}, u32[]{:S(2)}, u32[]{:S(2)}) collective-permute-start(bf16[272,128]{1,0:T(8,128)(2,1)S(1)} %get-tuple-element.15), channel_id=1, source_target_pairs={{0,960},{64,0},{128,64},{192,128},{256,192},{320,256},{384,320},{4... | collective-permute-start | bytes 208904 | tf_op jit(solution)/shard_map/ppermute | solution.py:28
  92.2 3.6 %copy-start.1 = (bf16[384,384]{1,0:T(8,128)(2,1)S(1)}, bf16[384,384]{1,0:T(8,128)(2,1)}, u32[]{:S(2)}) copy-start(bf16[384,384]{1,0:T(8,128)(2,1)} %param.9) | copy-start | bytes 884740
  136.4 2.0 copy-start
  136.4 2.0 copy-start.3
  139.0 1.3 copy-start.4
  139.0 1.3 copy-start.6
  139.0 1.3 copy-start.7

commit v5 on v1

--- a/solution.py
+++ b/solution.py
@@ -63,8 +63,19 @@
     seat_blocks, seat_cols = seat_layout(
         blocks, row_ids, col_ids, live_count, row_groups, seats_per_row
     )
-    owned_blocks = lax.all_to_all(seat_blocks, "row", split_axis=0, concat_axis=0, tiled=True)
-    owned_cols = lax.all_to_all(seat_cols, "row", split_axis=0, concat_axis=0, tiled=True)
+    block_len = blocks.shape[-1]
+    tail = 16
+    col_rows = jnp.broadcast_to(
+        seat_cols.astype(blocks.dtype)[:, :, None], (row_groups, seats_per_row, block_len)
+    )
+    col_rows = jnp.pad(col_rows, ((0, 0), (0, tail - seats_per_row), (0, 0)))
+    bundle = jnp.concatenate(
+        [seat_blocks.reshape(row_groups, seats_per_row * block_len, block_len), col_rows], axis=1
+    )
+    bundle = lax.all_to_all(bundle, "row", split_axis=0, concat_axis=0, tiled=True)
+    owned_blocks = bundle[:, : seats_per_row * block_len].reshape(seat_blocks.shape)
+    owned_cols = bundle[:, seats_per_row * block_len : seats_per_row * block_len + seats_per_row, 0]
+    owned_cols = owned_cols.astype(jnp.int32)
     hidden = to_grid(states)
     for iteration in range(ITERS):
         mixed = jnp.dot(hidden, mix_weight, preferred_element_type=jnp.float32).astype(jnp.bfloat16)

time: 185 us -> 181 us (0.978)
  blocking collectives: 62 us -> 102 us
  waiting for transfers between devices: 64.7 us -> 38.7 us
  starting transfers between devices: 14.9 us -> 0.04 us
  local copies, waits for them, and re-layouts: 17 us -> 13.5 us
    all_to_all x0 -> x1, blocking collectives: none -> 39.7 us  [body(): lax.all_to_all(bundle, 'row', split_axis=0, concat_axis=0, tiled=True)]
    all_gather x2, waiting for transfers between devices: 53.9 us -> 38.6 us  [couple(): pieces_all = lax.all_gather(grid_mixed, 'row', axis=0, tiled=False)]
    all_to_all x2 -> x0, starting transfers between devices: 14.8 us -> none  [the longest x1 7.6 us: body(): lax.all_to_all(seat_blocks, 'row', split_axis=0, concat_axis=0, tiled=True)]
    all_to_all x2 -> x0, waiting for transfers between devices: 10.8 us -> none  [the longest x1 10.8 us: body(): lax.all_to_all(seat_blocks, 'row', split_axis=0, concat_axis=0, tiled=True)]
    scatter x1, local copies, waits for them, and re-layouts: 4.65 us -> 1.78 us  [seat_layout(): seat_blocks = jnp.zeros((seat_total, block_len, block_len), blocks.dtype)...]
  transfers between devices with their start and end apart: 4 -> 2, of which waited for: 3 -> 1; matrix products, arithmetic and copies ran while one was open for 6% -> 3% of each run, Pallas kernels for 0% -> 0%
where the time goes in v5:
time: 181 us
  blocking collectives  102 us (56%)
  waiting for transfers between devices  38.7 us (21%)
  between operations  14.3 us (8%)
  local copies, waits for them, and re-layouts  13.5 us (7%)
  matrix products  8.01 us (4%)
  other arithmetic  4.33 us (2%)
    all_to_all x2, blocking collectives, to_grid(): lax.all_to_all(values, 'col', split_axis=0, concat_axis=0, tiled=True)  62 us
    all_to_all x1, blocking collectives, body(): lax.all_to_all(bundle, 'row', split_axis=0, concat_axis=0, tiled=True)  39.7 us
    all_gather x2, waiting for transfers between devices, couple(): pieces_all = lax.all_gather(grid_mixed, 'row', axis=0, tiled=False)  38.6 us
    gather x2, local copies, waits for them, and re-layouts, couple(): pieces = pieces_all[owned_cols]  5.28 us
    dot_general x2, matrix products, couple(): jnp.einsum('rsab,rsbh->rah', owned_blocks, pieces, preferred_element_type...  5.25 us
  transfers between devices with their start and end apart: 2, of which 1 were waited for; matrix products, arithmetic and copies ran while one was open for 3% of the time, Pallas kernels for 0%

profile of v5, /device:TPU:6, one launch (start us, length us, event | category | flops | bytes accessed | tf_op | source)
XLA Modules:
  0.0 180.7 jit_solution(2258497646419755176)
XLA Ops:
  6.5 0.0 copy-start
  6.5 0.0 copy-start.2
  6.5 0.0 all-gather.5.cloned.1.call-start
  6.5 1.0 all_to_all.17
  7.6 35.7 %all_to_all.26 = bf16[64,2,384]{2,1,0:T(2,128)(2,1)S(1)} all-to-all(bf16[64,2,384]{2,1,0:T(2,128)(2,1)S(1)} %all_to_all.17), channel_id=1, replica_groups=mesh['row'=16,'col'=64] {'col'}, dimensions={0} | all-to-all | bytes 196608 | tf_op jit(solution)/shard_map/all_to_all | solution.py:18
  43.3 0.0 copy-done
  43.3 0.0 copy-start.3
  43.3 0.9 convolution_convert_fusion.1
  44.2 0.0 all-gather.5.cloned.1.call-update
  44.2 0.0 all-gather.7.cloned.1.call-start
  44.9 0.9 convert_reduce_fusion.2
  45.8 0.7 fusion.10
  46.5 0.8 scatter_custom_fusion.1
  47.3 0.1 convert_element_type.68
  47.4 0.0 copy-done.3
  47.4 0.2 broadcast_in_dim.8
  47.6 0.0 copy-done.2
  47.6 1.8 scatter_fusion
  49.4 0.1 broadcast_in_dim.10
  49.5 0.1 fusion.1
  49.6 39.7 %all_to_all.27 = bf16[16,272,128]{2,1,0:T(8,128)(2,1)S(1)} all-to-all(bf16[16,272,128]{2,1,0:T(8,128)(2,1)S(1)} %fusion.1), channel_id=1, replica_groups=mesh['row'=16,'col'=64] {'row'}, dimensions={0} | all-to-all | bytes 2228224 | tf_op jit(solution)/shard_map/all_to_all | solution.py:75
  89.4 0.3 fusion.6
  89.7 0.1 reshape.200
  89.8 1.1 slice.12
  90.9 0.0 all-gather.5.cloned.1.call-done
  90.9 2.6 %gather_fusion = bf16[32,128,384]{2,1,0:T(8,128)(2,1)S(1)} fusion(bf16[16,128,384]{2,1,0:T(8,128)(2,1)} %bitcast.48, s32[1024]{0:T(1024)S(1)} %pad_clamp_fusion), kind=kCustom, calls=%fused_computation | custom fusion | bytes 6291584 | tf_op jit(solution)/shard_map/gather | solution.py:48
  93.5 0.0 copy-start.6
  93.5 0.0 copy-start.7
  93.5 2.6 %convert_reduce_fusion.1 = f32[128,384]{1,0:T(8,128)} fusion(bf16[16,2,128,128]{3,2,1,0:T(8,128)(2,1)} %bitcast.46, bf16[16,2,128,384]{3,2,1,0:T(8,128)(2,1)S(1)} %bitcast.44), kind=kOutput, calls=%fused_computation.7 | convolution fusion | flops 404963328 | bytes 4390912 | tf_op jit(solution)/shard_map/rsab,rsbh->rah/dot_general | solution.py:49
  96.2 1.0 reduce_sum.72
  97.2 0.0 copy-start.1
  97.2 0.2 fusion.9
  97.4 0.0 copy-start.4
  97.4 0.1 div.16
  97.6 0.3 multiply_reduce_fusion.1
  97.9 0.0 copy-start.5
  97.9 0.1 rsqrt.21
  98.0 0.0 copy-done.6
  98.0 0.0 copy-done.7
  98.0 1.9 %convolution_convert_fusion = bf16[128,384]{1,0:T(8,128)(2,1)} fusion(bf16[384,384]{1,0:T(8,128)(2,1)S(1)} %copy-done, f32[128,384]{1,0:T(8,128)} %convert_reduce_fusion.1, bf16[128,384]{1,0:T(8,128)(2,1)} %copy-done.3, f32[384]{0:T(512)S(1)} %copy-done.6, f32[384]{0:T(512)S(1)} %copy-done.7, f32[128]{0:T(128)S(1)} %rsqrt.21, f32[128]{0:T(128)S(1)} %div.16), kind=kOutput, calls=%fused_computation.10 | convolution fusion | flops 38141952 | bytes 692224 | tf_op jit(solution)/shard_map/dot_general | solution.py:81
  99.9 0.0 all-gather.7.cloned.1.call-update
  100.0 38.6 %all-gather.7.cloned.1.call-done = bf16[2048,384]{1,0:T(8,128)(2,1)} async-done(((bf16[128,384]{1,0:T(8,128)(2,1)}), bf16[2048,384]{1,0:T(8,128)(2,1)}) %all-gather.7.cloned.1.call-update) | async-done | bytes 1572880 | tf_op jit(solution)/shard_map/all_gather | solution.py:47
  138.6 0.0 copy-done.1
  138.6 0.0 copy-done.4
  138.6 0.0 copy-done.5
  138.6 2.6 %gather_fusion.1 = bf16[32,128,384]{2,1,0:T(8,128)(2,1)S(1)} fusion(bf16[16,128,384]{2,1,0:T(8,128)(2,1)} %bitcast.49, s32[1024]{0:T(1024)S(1)} %pad_clamp_fusion), kind=kCustom, calls=%fused_computation.1 | custom fusion | bytes 6291584 | tf_op jit(solution)/shard_map/gather | solution.py:48
  141.2 2.6 %convert_reduce_fusion = f32[128,384]{1,0:T(8,128)} fusion(bf16[16,2,128,128]{3,2,1,0:T(8,128)(2,1)} %bitcast.47, bf16[16,2,128,384]{3,2,1,0:T(8,128)(2,1)S(1)} %bitcast.43), kind=kOutput, calls=%fused_computation.6 | convolution fusion | flops 404963328 | bytes 4390912 | tf_op jit(solution)/shard_map/rsab,rsbh->rah/dot_general | solution.py:49
  143.9 1.0 reduce_sum.76
  144.9 1.4 fusion.13
  146.3 0.2 multiply_reduce_fusion
  146.6 0.2 add_convert_fusion
  146.8 26.4 %all_to_all.28 = bf16[64,2,384]{2,1,0:T(2,128)(2,1)S(1)} all-to-all(bf16[64,2,384]{2,1,0:T(2,128)(2,1)S(1)} %add_convert_fusion), channel_id=1, replica_groups=mesh['row'=16,'col'=64] {'col'}, dimensions={0} | all-to-all | bytes 196608 | tf_op jit(solution)/shard_map/all_to_all | solution.py:18
  173.2 0.7 all_to_all.22
  (8 shorter events, 0.1 us)
Async XLA Ops:
  6.5 36.8 %copy-start = (bf16[384,384]{1,0:T(8,128)(2,1)S(1)}, bf16[384,384]{1,0:T(8,128)(2,1)}, u32[]{:S(2)}) copy-start(bf16[384,384]{1,0:T(8,128)(2,1)} %param.9) | copy-start | bytes 884740
  6.5 41.1 %copy-start.2 = (bf16[1,1,32,128,128]{4,3,2,1,0:T(8,128)(2,1)S(1)}, bf16[1,1,32,128,128]{4,3,2,1,0:T(8,128)(2,1)}, u32[]{:S(2)}) copy-start(bf16[1,1,32,128,128]{4,3,2,1,0:T(8,128)(2,1)} %param.10) | copy-start | bytes 3145732
  6.5 84.3 %all-gather.5.cloned.1.call-start = ((), (), s32[]{:S(2)}) async-start(), calls=%async_computation.3 | async-start | bytes 1671168 | tf_op jit(solution)/shard_map/all_gather | solution.py:47
  43.3 4.1 %copy-start.3 = (bf16[128,384]{1,0:T(8,128)(2,1)}, bf16[128,384]{1,0:T(8,128)(2,1)S(1)}, u32[]{:S(2)}) copy-start(bf16[128,384]{1,0:T(8,128)(2,1)S(1)} %all_to_all.20) | copy-start | bytes 294916
  44.2 94.4 %all-gather.7.cloned.1.call-start = ((), (), s32[]{:S(2)}) async-start(), calls=%async_computation.4 | async-start | bytes 1671168 | tf_op jit(solution)/shard_map/all_gather | solution.py:47
  93.5 4.5 %copy-start.6 = (f32[384]{0:T(512)S(1)}, f32[384]{0:T(512)}, u32[]{:S(2)}) copy-start(f32[384]{0:T(512)} %param.15) | copy-start | bytes 4612
  93.5 4.5 %copy-start.7 = (f32[384]{0:T(512)S(1)}, f32[384]{0:T(512)}, u32[]{:S(2)}) copy-start(f32[384]{0:T(512)} %param.14) | copy-start | bytes 4612
  97.2 41.4 %copy-start.1 = (f32[64,2,384]{2,1,0:T(2,128)}, f32[64,2,384]{2,1,0:T(2,128)S(1)}, u32[]{:S(2)}) copy-start(f32[64,2,384]{2,1,0:T(2,128)S(1)} %reduce_sum.72) | copy-start | bytes 589828
  97.4 41.2 %copy-start.4 = (f32[64,2]{1,0:T(8,128)}, f32[64,2]{1,0:T(8,128)S(1)}, u32[]{:S(2)}) copy-start(f32[64,2]{1,0:T(8,128)S(1)} %broadcast_multiply_fusion.1) | copy-start | bytes 1540
  97.9 40.7 %copy-start.5 = (f32[64,2]{1,0:T(8,128)}, f32[64,2]{1,0:T(8,128)S(1)}, u32[]{:S(2)}) copy-start(f32[64,2]{1,0:T(8,128)S(1)} %add_rsqrt_fusion.1) | copy-start | bytes 1540
Sparse Core Ops, SparseCore 0:
  44.3 42.5 all-gather.4
  100.1 38.4 all-gather.6

commit v6 on v5

--- a/solution.py
+++ b/solution.py
@@ -1,6 +1,8 @@
 import jax
 import jax.numpy as jnp
 from jax import lax
+from jax.experimental import pallas as pl
+from jax.experimental.pallas import tpu as pltpu
 from jax.sharding import PartitionSpec as P
 
 ITERS = 2
@@ -52,6 +54,47 @@
     return jnp.sum(per_source.astype(jnp.bfloat16).astype(jnp.float32), axis=0)
 
 
+def couple_kernel(cols_ref, blocks_ref, pieces_ref, hidden_ref, weight_ref, gain_ref, bias_ref,
+                  hidden_out, mixed_out):
+    sources, seats = blocks_ref.shape[0], blocks_ref.shape[1]
+
+    def source_term(source, total):
+        term = None
+        for seat in range(seats):
+            piece = pieces_ref[cols_ref[source * seats + seat]]
+            product = jnp.dot(blocks_ref[source, seat], piece, preferred_element_type=jnp.float32)
+            term = product if term is None else term + product
+        return total + term.astype(jnp.bfloat16).astype(jnp.float32)
+
+    coupled = lax.fori_loop(0, sources, source_term, jnp.zeros(hidden_ref.shape, jnp.float32))
+    hidden = normalize(hidden_ref[...], coupled, gain_ref[...], bias_ref[...])
+    hidden_out[...] = hidden
+    mixed_out[...] = jnp.dot(
+        hidden, weight_ref[...], preferred_element_type=jnp.float32
+    ).astype(jnp.bfloat16)
+
+
+def couple_step(pieces_all, owned_blocks, owned_cols, hidden, mix_weight, gain, bias):
+    vmem = pl.BlockSpec(memory_space=pltpu.VMEM)
+    return pl.pallas_call(
+        couple_kernel,
+        out_shape=(
+            jax.ShapeDtypeStruct(hidden.shape, jnp.bfloat16),
+            jax.ShapeDtypeStruct(hidden.shape, jnp.bfloat16),
+        ),
+        in_specs=[pl.BlockSpec(memory_space=pltpu.SMEM)] + [vmem] * 6,
+        out_specs=(vmem, vmem),
+    )(
+        owned_cols.reshape(-1),
+        owned_blocks,
+        pieces_all,
+        hidden,
+        mix_weight,
+        gain.reshape(1, -1),
+        bias.reshape(1, -1),
+    )
+
+
 def body(states, mix_weight, coherence, block_row, block_col, block_count, gain, bias):
     blocks = coherence[0, 0]
     row_ids = block_row[0, 0]
@@ -77,10 +120,12 @@
     owned_cols = bundle[:, seats_per_row * block_len : seats_per_row * block_len + seats_per_row, 0]
     owned_cols = owned_cols.astype(jnp.int32)
     hidden = to_grid(states)
+    mixed = jnp.dot(hidden, mix_weight, preferred_element_type=jnp.float32).astype(jnp.bfloat16)
     for iteration in range(ITERS):
-        mixed = jnp.dot(hidden, mix_weight, preferred_element_type=jnp.float32).astype(jnp.bfloat16)
-        coupled = couple(mixed, owned_blocks, owned_cols)
-        hidden = normalize(hidden, coupled, gain, bias)
+        pieces_all = lax.all_gather(mixed, "row", axis=0, tiled=False)
+        hidden, mixed = couple_step(
+            pieces_all, owned_blocks, owned_cols, hidden, mix_weight, gain, bias
+        )
     return to_grid(hidden)
 
 

time: 181 us -> 180 us (level)
  blocking collectives: 102 us -> 62.1 us
  waiting for transfers between devices: 38.7 us -> 72 us
  Pallas kernels: 0 us -> 12.3 us
  starting transfers between devices: 0.04 us -> 7.44 us
  matrix products: 8.01 us -> 1.85 us
  local copies, waits for them, and re-layouts: 13.5 us -> 8.49 us
  other arithmetic: 4.33 us -> 1.62 us
    all_to_all x1 -> x0, blocking collectives: 39.7 us -> none  [body(): lax.all_to_all(bundle, 'row', split_axis=0, concat_axis=0, tiled=True)]
    all_to_all x0 -> x1, waiting for transfers between devices: none -> 31.6 us  [body(): lax.all_to_all(bundle, 'row', split_axis=0, concat_axis=0, tiled=True)]
    pallas_call x0 -> x2, Pallas kernels: none -> 12.3 us  [couple_step(): pl.pallas_call(couple_kernel, out_shape=(jax.ShapeDtypeStruct(hidden.shap...]
    all_to_all x0 -> x1, starting transfers between devices: none -> 7.4 us  [body(): lax.all_to_all(bundle, 'row', split_axis=0, concat_axis=0, tiled=True)]
    gather x2 -> x0, local copies, waits for them, and re-layouts: 5.28 us -> none  [couple(): pieces = pieces_all[owned_cols]]
    dot_general x2 -> x0, matrix products: 5.25 us -> none  [couple(): jnp.einsum('rsab,rsbh->rah', owned_blocks, pieces, preferred_element_type...]
    reduce_sum x2 -> x0, local copies, waits for them, and re-layouts: 2.07 us -> none  [couple(): return jnp.sum(per_source.astype(jnp.bfloat16).astype(jnp.float32), axis=0)]
    reduce_sum x4 -> x0, other arithmetic: 2.05 us -> none  [the longest x2 1.53 us: normalize(): mean_value = jnp.mean(summed_in, axis=-1, keepdims=True)]
  transfers between devices with their start and end apart: 2 -> 3, of which waited for: 1 -> 2; matrix products, arithmetic and copies ran while one was open for 3% -> 4% of each run, Pallas kernels for 0% -> 0%
where the time goes in v6:
time: 180 us
  waiting for transfers between devices  72 us (40%)
  blocking collectives  62.1 us (34%)
  between operations  14.2 us (8%)
  Pallas kernels  12.3 us (7%)
  local copies, waits for them, and re-layouts  8.49 us (5%)
  starting transfers between devices  7.44 us (4%)
  matrix products  1.85 us (1%)
    all_to_all x2, blocking collectives, to_grid(): lax.all_to_all(values, 'col', split_axis=0, concat_axis=0, tiled=True)  62.1 us
    all_gather x2, waiting for transfers between devices, body(): pieces_all = lax.all_gather(mixed, 'row', axis=0, tiled=False)  40.4 us
    all_to_all x1, waiting for transfers between devices, body(): lax.all_to_all(bundle, 'row', split_axis=0, concat_axis=0, tiled=True)  31.6 us
    pallas_call x2, Pallas kernels, couple_step(): pl.pallas_call(couple_kernel, out_shape=(jax.ShapeDtypeStruct(hidden.shap...  12.3 us
    all_to_all x1, starting transfers between devices, body(): lax.all_to_all(bundle, 'row', split_axis=0, concat_axis=0, tiled=True)  7.4 us
  transfers between devices with their start and end apart: 3, of which 2 were waited for; matrix products, arithmetic and copies ran while one was open for 4% of the time, Pallas kernels for 0%

profile of v6, /device:TPU:6, one launch (start us, length us, event | category | flops | bytes accessed | tf_op | source)
XLA Modules:
  0.0 180.0 jit_solution(15605531043524085778)
XLA Ops:
  6.5 0.0 copy-start.2
  6.5 0.0 copy-start
  6.5 0.0 all-gather.5.cloned.1.call-start
  6.5 1.0 all_to_all.19
  7.6 35.7 %all_to_all.28 = bf16[64,2,384]{2,1,0:T(2,128)(2,1)S(1)} all-to-all(bf16[64,2,384]{2,1,0:T(2,128)(2,1)S(1)} %all_to_all.19), channel_id=1, replica_groups=mesh['row'=16,'col'=64] {'col'}, dimensions={0} | all-to-all | bytes 196608 | tf_op jit(solution)/shard_map/all_to_all | solution.py:20
  43.3 0.0 copy-start.1
  43.3 1.9 %convolution_convert_fusion = bf16[128,384]{1,0:T(8,128)(2,1)} fusion(bf16[128,384]{1,0:T(8,128)(2,1)S(1)} %all_to_all.21.hidden_ref, bf16[384,384]{1,0:T(8,128)(2,1)} %weight_ref.3), kind=kOutput, calls=%fused_computation.4 | convolution fusion | flops 37797888 | bytes 491520 | tf_op jit(solution)/shard_map/dot_general | solution.py:123
  45.1 0.0 all-gather.5.cloned.1.call-update
  45.8 0.0 copy-done.2
  45.8 0.2 convert_reduce_fusion.1
  46.0 0.8 scatter_custom_fusion.1
  46.8 0.1 convert_element_type.27
  46.9 0.2 broadcast_in_dim.8
  47.2 0.0 copy-done
  47.2 1.7 scatter_fusion
  48.9 0.0 copy-done.1
  48.9 0.1 broadcast_in_dim.10
  49.0 1.1 fusion.1
  50.1 0.0 copy-start.3
  50.1 0.0 copy-start.4
  50.1 7.4 %all-to-all-start = ((bf16[16,272,128]{2,1,0:T(8,128)(2,1)}), bf16[16,272,128]{2,1,0:T(8,128)(2,1)S(1)}, u32[]{:S(2)}, u32[]{:S(2)}) async-start(bf16[16,272,128]{2,1,0:T(8,128)(2,1)} %fusion.1), calls=%async_computation | async-start | bytes 2228224 | tf_op jit(solution)/shard_map/all_to_all | solution.py:118
  57.5 0.0 all-gather.7.cloned.1.call-start
  57.6 0.0 copy-done.3
  57.6 0.5 reshape.72.gain_ref
  58.1 0.0 copy-done.4
  58.1 0.6 reshape.73.bias_ref
  58.7 31.6 %all-to-all-done = bf16[16,272,128]{2,1,0:T(8,128)(2,1)S(1)} async-done(((bf16[16,272,128]{2,1,0:T(8,128)(2,1)}), bf16[16,272,128]{2,1,0:T(8,128)(2,1)S(1)}, u32[]{:S(2)}, u32[]{:S(2)}) %all-to-all-start) | async-done | bytes 1114144 | tf_op jit(solution)/shard_map/all_to_all | solution.py:118
  90.3 0.3 convert_reduce_fusion
  90.6 0.7 reshape.74.cols_ref
  91.3 1.1 slice.9
  92.3 0.0 all-gather.5.cloned.1.call-done
  92.3 6.2 %shard_map.82 = (bf16[128,384]{1,0:T(8,128)(2,1)}, bf16[128,384]{1,0:T(8,128)(2,1)}) custom-call(s32[32]{0:T(128)} %reshape.74.cols_ref, bf16[16,2,128,128]{3,2,1,0:T(8,128)(2,1)} %bitcast.24, bf16[16,128,384]{2,1,0:T(8,128)(2,1)} %bitcast.27, bf16[128,384]{1,0:T(8,128)(2,1)} %copy-done.1, bf16[384,384]{1,0:T(8,128)(2,1)} %weight_ref.3, ...), custom_call_target="tpu_custom_call" | custom-call | tf_op jit(solution)/shard_map/pallas_call | solution.py:79
  98.5 0.0 all-gather.7.cloned.1.call-update
  98.5 40.4 %all-gather.7.cloned.1.call-done = bf16[2048,384]{1,0:T(8,128)(2,1)} async-done(((bf16[128,384]{1,0:T(8,128)(2,1)}), bf16[2048,384]{1,0:T(8,128)(2,1)}) %all-gather.7.cloned.1.call-update) | async-done | bytes 1572880 | tf_op jit(solution)/shard_map/all_gather | solution.py:125
  138.9 6.2 %shard_map.83 = (bf16[128,384]{1,0:T(8,128)(2,1)}, bf16[128,384]{1,0:T(8,128)(2,1)}) custom-call(s32[32]{0:T(128)} %reshape.74.cols_ref, bf16[16,2,128,128]{3,2,1,0:T(8,128)(2,1)} %bitcast.25, bf16[16,128,384]{2,1,0:T(8,128)(2,1)} %bitcast.28, bf16[128,384]{1,0:T(8,128)(2,1)} %get-tuple-element.9.hidden_ref, bf16[384,384]{1,0:T(8,128)(2,1)} %weight_ref.3, ...), custom_call_target="tpu_custom_call" | custom-call | tf_op jit(solution)/shard_map/pallas_call | solution.py:79
  145.1 0.9 all_to_all.22
  146.1 26.4 %all_to_all.29 = bf16[64,2,384]{2,1,0:T(2,128)(2,1)S(1)} all-to-all(bf16[64,2,384]{2,1,0:T(2,128)(2,1)S(1)} %all_to_all.22), channel_id=1, replica_groups=mesh['row'=16,'col'=64] {'col'}, dimensions={0} | all-to-all | bytes 196608 | tf_op jit(solution)/shard_map/all_to_all | solution.py:20
  172.4 0.7 all_to_all.24
  (4 shorter events, 0.1 us)
Async XLA Ops:
  6.5 39.3 %copy-start.2 = (s32[1,1,32]{2,1,0:T(1,128)S(1)}, s32[1,1,32]{2,1,0:T(1,128)}, u32[]{:S(2)}) copy-start(s32[1,1,32]{2,1,0:T(1,128)} %param.11) | copy-start | bytes 388
  6.5 40.6 %copy-start = (bf16[1,1,32,128,128]{4,3,2,1,0:T(8,128)(2,1)S(1)}, bf16[1,1,32,128,128]{4,3,2,1,0:T(8,128)(2,1)}, u32[]{:S(2)}) copy-start(bf16[1,1,32,128,128]{4,3,2,1,0:T(8,128)(2,1)} %param.10) | copy-start | bytes 3145732
  6.5 85.8 %all-gather.5.cloned.1.call-start = ((), (), s32[]{:S(2)}) async-start(), calls=%async_computation.3 | async-start | bytes 1671168 | tf_op jit(solution)/shard_map/all_gather | solution.py:125
  43.3 5.7 %copy-start.1 = (bf16[128,384]{1,0:T(8,128)(2,1)}, bf16[128,384]{1,0:T(8,128)(2,1)S(1)}, u32[]{:S(2)}) copy-start(bf16[128,384]{1,0:T(8,128)(2,1)S(1)} %all_to_all.21.hidden_ref) | copy-start | bytes 294916
  50.1 7.4 %copy-start.3 = (f32[384]{0:T(512)S(1)}, f32[384]{0:T(512)}, u32[]{:S(2)}) copy-start(f32[384]{0:T(512)} %param.14) | copy-start | bytes 4612
  50.1 8.0 %copy-start.4 = (f32[384]{0:T(512)S(1)}, f32[384]{0:T(512)}, u32[]{:S(2)}) copy-start(f32[384]{0:T(512)} %param.15) | copy-start | bytes 4612
  50.1 40.1 %all-to-all-start = ((bf16[16,272,128]{2,1,0:T(8,128)(2,1)}), bf16[16,272,128]{2,1,0:T(8,128)(2,1)S(1)}, u32[]{:S(2)}, u32[]{:S(2)}) async-start(bf16[16,272,128]{2,1,0:T(8,128)(2,1)} %fusion.1), calls=%async_computation | async-start | bytes 2228224 | tf_op jit(solution)/shard_map/all_to_all | solution.py:118
  57.5 81.4 %all-gather.7.cloned.1.call-start = ((), (), s32[]{:S(2)}) async-start(), calls=%async_computation.4 | async-start | bytes 1671168 | tf_op jit(solution)/shard_map/all_gather | solution.py:125
Sparse Core Ops, SparseCore 0:
  45.3 44.6 all-gather.4
  98.6 40.2 all-gather.6

commit v7 on v6

--- a/solution.py
+++ b/solution.py
@@ -122,7 +122,17 @@
     hidden = to_grid(states)
     mixed = jnp.dot(hidden, mix_weight, preferred_element_type=jnp.float32).astype(jnp.bfloat16)
     for iteration in range(ITERS):
-        pieces_all = lax.all_gather(mixed, "row", axis=0, tiled=False)
+        if iteration == 0:
+            pieces_all = lax.all_gather(mixed, "row", axis=0, tiled=False)
+        else:
+            half = mixed.shape[-1] // 2
+            pieces_all = jnp.concatenate(
+                [
+                    lax.all_gather(mixed[:, :half], "row", axis=0, tiled=False),
+                    lax.all_gather(mixed[:, half:], "row", axis=0, tiled=False),
+                ],
+                axis=-1,
+            )
         hidden, mixed = couple_step(
             pieces_all, owned_blocks, owned_cols, hidden, mix_weight, gain, bias
         )

time: 180 us -> 177 us (0.983)
  the two profiles are of different devices: /device:TPU:6 before, /device:TPU:2 now
where the time goes in v7:
time: 177 us; the launch traced here: 176 us
  blocking collectives  96.1 us (54%)
  waiting for transfers between devices  30 us (17%)
  between operations  14.1 us (8%)
  Pallas kernels  12.3 us (7%)
  local copies, waits for them, and re-layouts  9.47 us (5%)
  starting transfers between devices  7.46 us (4%)
  other arithmetic  4.84 us (3%)
  matrix products  1.85 us (1%)
    all_to_all x2, blocking collectives, to_grid(): lax.all_to_all(values, 'col', split_axis=0, concat_axis=0, tiled=True)  58.6 us
    all_to_all x1, waiting for transfers between devices, body(): lax.all_to_all(bundle, 'row', split_axis=0, concat_axis=0, tiled=True)  30 us
    all_gather x1, blocking collectives, body(): lax.all_gather(mixed[:, :half], 'row', axis=0, tiled=False)  19 us
    all_gather x1, blocking collectives, body(): lax.all_gather(mixed[:, half:], 'row', axis=0, tiled=False)  18.5 us
    pallas_call x2, Pallas kernels, couple_step(): pl.pallas_call(couple_kernel, out_shape=(jax.ShapeDtypeStruct(hidden.shap...  12.3 us
    all_to_all x1, starting transfers between devices, body(): lax.all_to_all(bundle, 'row', split_axis=0, concat_axis=0, tiled=True)  7.46 us
  transfers between devices with their start and end apart: 2, of which 1 were waited for; matrix products, arithmetic and copies ran while one was open for 5% of the time, Pallas kernels for 0%

profile of v7, /device:TPU:2, one launch (start us, length us, event | category | flops | bytes accessed | tf_op | source)
XLA Modules:
  0.0 176.2 jit_solution(17405562002565671017)
XLA Ops:
  6.5 0.0 copy-start
  6.5 0.0 all-gather.5.cloned.1.call-start
  6.5 1.0 all_to_all.19
  7.6 35.7 %all_to_all.28 = bf16[64,2,384]{2,1,0:T(2,128)(2,1)S(1)} all-to-all(bf16[64,2,384]{2,1,0:T(2,128)(2,1)S(1)} %all_to_all.19), channel_id=1, replica_groups=mesh['row'=16,'col'=64] {'col'}, dimensions={0} | all-to-all | bytes 196608 | tf_op jit(solution)/shard_map/all_to_all | solution.py:20
  43.3 0.0 copy-start.1
  43.3 1.8 %convolution_convert_fusion = bf16[128,384]{1,0:T(8,128)(2,1)} fusion(bf16[128,384]{1,0:T(8,128)(2,1)S(1)} %all_to_all.21.hidden_ref, bf16[384,384]{1,0:T(8,128)(2,1)} %weight_ref.3), kind=kOutput, calls=%fused_computation.5 | convolution fusion | flops 37797888 | bytes 491520 | tf_op jit(solution)/shard_map/dot_general | solution.py:123
  45.1 0.0 all-gather.5.cloned.1.call-update
  45.8 0.9 convert_reduce_fusion.1
  46.7 0.7 fusion.4
  47.4 0.8 scatter_custom_fusion.1
  48.2 0.1 convert_element_type.27
  48.3 0.2 broadcast_in_dim.8
  48.5 0.0 copy-done
  48.6 1.8 scatter_fusion
  50.3 0.0 copy-done.1
  50.3 0.1 broadcast_in_dim.10
  50.4 1.1 fusion.1
  51.5 0.0 copy-start.2
  51.5 0.0 copy-start.3
  51.5 7.5 %all-to-all-start = ((bf16[16,272,128]{2,1,0:T(8,128)(2,1)}), bf16[16,272,128]{2,1,0:T(8,128)(2,1)S(1)}, u32[]{:S(2)}, u32[]{:S(2)}) async-start(bf16[16,272,128]{2,1,0:T(8,128)(2,1)} %fusion.1), calls=%async_computation | async-start | bytes 2228224 | tf_op jit(solution)/shard_map/all_to_all | solution.py:118
  59.0 0.0 copy-done.2
  59.0 0.6 reshape.72.gain_ref
  59.5 0.0 copy-done.3
  59.6 0.5 reshape.73.bias_ref
  60.1 30.0 %all-to-all-done = bf16[16,272,128]{2,1,0:T(8,128)(2,1)S(1)} async-done(((bf16[16,272,128]{2,1,0:T(8,128)(2,1)}), bf16[16,272,128]{2,1,0:T(8,128)(2,1)S(1)}, u32[]{:S(2)}, u32[]{:S(2)}) %all-to-all-start) | async-done | bytes 1114144 | tf_op jit(solution)/shard_map/all_to_all | solution.py:118
  90.1 0.3 convert_reduce_fusion
  90.4 0.6 reshape.74.cols_ref
  91.0 1.1 slice.17
  92.1 0.0 all-gather.5.cloned.1.call-done
  92.1 6.2 %shard_map.82 = (bf16[128,384]{1,0:T(8,128)(2,1)}, bf16[128,384]{1,0:T(8,128)(2,1)}) custom-call(s32[32]{0:T(128)} %reshape.74.cols_ref, bf16[16,2,128,128]{3,2,1,0:T(8,128)(2,1)} %bitcast.27, bf16[16,128,384]{2,1,0:T(8,128)(2,1)} %bitcast.32, bf16[128,384]{1,0:T(8,128)(2,1)} %copy-done.1, bf16[384,384]{1,0:T(8,128)(2,1)} %weight_ref.3, ...), custom_call_target="tpu_custom_call" | custom-call | tf_op jit(solution)/shard_map/pallas_call | solution.py:79
  98.3 1.0 fusion.7
  99.3 19.0 %all-gather.1 = bf16[2048,192]{1,0:T(8,128)(2,1)S(1)} all-gather(bf16[128,192]{1,0:T(8,128)(2,1)S(1)} %get-tuple-element.11), channel_id=3, replica_groups=mesh['row'=16,'col'=64] {'row'}, dimensions={0}, use_global_device_ids=true | all-gather | bytes 835584 | tf_op jit(solution)/shard_map/all_gather | solution.py:131
  118.3 18.5 %all-gather.2 = bf16[2048,192]{1,0:T(8,128)(2,1)S(1)} all-gather(bf16[128,192]{1,0:T(8,128)(2,1)S(1)} %get-tuple-element.12), channel_id=4, replica_groups=mesh['row'=16,'col'=64] {'row'}, dimensions={0}, use_global_device_ids=true | all-gather | bytes 835584 | tf_op jit(solution)/shard_map/all_gather | solution.py:132
  136.8 1.8 %pad_maximum_fusion.pieces_ref = bf16[16,128,384]{2,1,0:T(8,128)(2,1)} fusion(bf16[16,128,192]{2,1,0:T(8,128)(2,1)S(1)} %bitcast.31, bf16[16,128,192]{2,1,0:T(8,128)(2,1)S(1)} %bitcast.30), kind=kLoop, calls=%fused_computation.4 | loop fusion | flops 3145728 | bytes 3145728 | tf_op jit(solution)/shard_map/concatenate | solution.py:129
  138.6 6.2 %shard_map.83 = (bf16[128,384]{1,0:T(8,128)(2,1)}, bf16[128,384]{1,0:T(8,128)(2,1)}) custom-call(s32[32]{0:T(128)} %reshape.74.cols_ref, bf16[16,2,128,128]{3,2,1,0:T(8,128)(2,1)} %bitcast.28, bf16[16,128,384]{2,1,0:T(8,128)(2,1)} %pad_maximum_fusion.pieces_ref, bf16[128,384]{1,0:T(8,128)(2,1)} %get-tuple-element.9.hidden_ref, bf16[384,384]{1,0:T(8,128)(2,1)} %weight_ref.3, ...), custom_call_target="tpu_custom_call" | custom-call | tf_op jit(solution)/shard_map/pallas_call | solution.py:79
  144.8 0.9 all_to_all.22
  145.7 22.9 %all_to_all.29 = bf16[64,2,384]{2,1,0:T(2,128)(2,1)S(1)} all-to-all(bf16[64,2,384]{2,1,0:T(2,128)(2,1)S(1)} %all_to_all.22), channel_id=1, replica_groups=mesh['row'=16,'col'=64] {'col'}, dimensions={0} | all-to-all | bytes 196608 | tf_op jit(solution)/shard_map/all_to_all | solution.py:20
  168.6 0.7 all_to_all.24
  (3 shorter events, 0.1 us)
Async XLA Ops:
  6.5 42.0 %copy-start = (bf16[1,1,32,128,128]{4,3,2,1,0:T(8,128)(2,1)S(1)}, bf16[1,1,32,128,128]{4,3,2,1,0:T(8,128)(2,1)}, u32[]{:S(2)}) copy-start(bf16[1,1,32,128,128]{4,3,2,1,0:T(8,128)(2,1)} %param.10) | copy-start | bytes 3145732
  6.5 85.6 %all-gather.5.cloned.1.call-start = ((), (), s32[]{:S(2)}) async-start(), calls=%async_computation.3 | async-start | bytes 1671168 | tf_op jit(solution)/shard_map/all_gather | solution.py:126
  43.3 7.1 %copy-start.1 = (bf16[128,384]{1,0:T(8,128)(2,1)}, bf16[128,384]{1,0:T(8,128)(2,1)S(1)}, u32[]{:S(2)}) copy-start(bf16[128,384]{1,0:T(8,128)(2,1)S(1)} %all_to_all.21.hidden_ref) | copy-start | bytes 294916
  51.5 7.5 %copy-start.2 = (f32[384]{0:T(512)S(1)}, f32[384]{0:T(512)}, u32[]{:S(2)}) copy-start(f32[384]{0:T(512)} %param.14) | copy-start | bytes 4612
  51.5 8.0 %copy-start.3 = (f32[384]{0:T(512)S(1)}, f32[384]{0:T(512)}, u32[]{:S(2)}) copy-start(f32[384]{0:T(512)} %param.15) | copy-start | bytes 4612
  51.5 38.6 %all-to-all-start = ((bf16[16,272,128]{2,1,0:T(8,128)(2,1)}), bf16[16,272,128]{2,1,0:T(8,128)(2,1)S(1)}, u32[]{:S(2)}, u32[]{:S(2)}) async-start(bf16[16,272,128]{2,1,0:T(8,128)(2,1)} %fusion.1), calls=%async_computation | async-start | bytes 2228224 | tf_op jit(solution)/shard_map/all_to_all | solution.py:118
Sparse Core Ops, SparseCore 0:
  45.3 44.6 all-gather.4

commit v8 on v7

--- a/solution.py
+++ b/solution.py
@@ -54,45 +54,48 @@
     return jnp.sum(per_source.astype(jnp.bfloat16).astype(jnp.float32), axis=0)
 
 
-def couple_kernel(cols_ref, blocks_ref, pieces_ref, hidden_ref, weight_ref, gain_ref, bias_ref,
-                  hidden_out, mixed_out):
-    sources, seats = blocks_ref.shape[0], blocks_ref.shape[1]
+def couple_kernel(cols_ref, bundle_ref, pieces_ref, hidden_ref, weight_ref, gain_ref, bias_ref,
+                  hidden_out, *mixed_out):
+    sources = bundle_ref.shape[0]
+    block_len = hidden_ref.shape[0]
+    seats = cols_ref.shape[0] // sources
 
     def source_term(source, total):
         term = None
         for seat in range(seats):
             piece = pieces_ref[cols_ref[source * seats + seat]]
-            product = jnp.dot(blocks_ref[source, seat], piece, preferred_element_type=jnp.float32)
+            block = bundle_ref[source, seat * block_len:(seat + 1) * block_len, :]
+            product = jnp.dot(block, piece, preferred_element_type=jnp.float32)
             term = product if term is None else term + product
         return total + term.astype(jnp.bfloat16).astype(jnp.float32)
 
     coupled = lax.fori_loop(0, sources, source_term, jnp.zeros(hidden_ref.shape, jnp.float32))
     hidden = normalize(hidden_ref[...], coupled, gain_ref[...], bias_ref[...])
     hidden_out[...] = hidden
-    mixed_out[...] = jnp.dot(
-        hidden, weight_ref[...], preferred_element_type=jnp.float32
-    ).astype(jnp.bfloat16)
+    for out in mixed_out:
+        out[...] = jnp.dot(hidden, weight_ref[...], preferred_element_type=jnp.float32).astype(
+            jnp.bfloat16
+        )
 
 
-def couple_step(pieces_all, owned_blocks, owned_cols, hidden, mix_weight, gain, bias):
+def couple_step(pieces_all, bundle, owned_cols, hidden, mix_weight, gain, bias, mix_next):
     vmem = pl.BlockSpec(memory_space=pltpu.VMEM)
-    return pl.pallas_call(
+    outs = 2 if mix_next else 1
+    results = pl.pallas_call(
         couple_kernel,
-        out_shape=(
-            jax.ShapeDtypeStruct(hidden.shape, jnp.bfloat16),
-            jax.ShapeDtypeStruct(hidden.shape, jnp.bfloat16),
-        ),
+        out_shape=tuple(jax.ShapeDtypeStruct(hidden.shape, jnp.bfloat16) for _ in range(outs)),
         in_specs=[pl.BlockSpec(memory_space=pltpu.SMEM)] + [vmem] * 6,
-        out_specs=(vmem, vmem),
+        out_specs=tuple(vmem for _ in range(outs)),
     )(
         owned_cols.reshape(-1),
-        owned_blocks,
+        bundle,
         pieces_all,
         hidden,
         mix_weight,
         gain.reshape(1, -1),
         bias.reshape(1, -1),
     )
+    return results if mix_next else (results[0], None)
 
 
 def body(states, mix_weight, coherence, block_row, block_col, block_count, gain, bias):
@@ -116,7 +119,6 @@
         [seat_blocks.reshape(row_groups, seats_per_row * block_len, block_len), col_rows], axis=1
     )
     bundle = lax.all_to_all(bundle, "row", split_axis=0, concat_axis=0, tiled=True)
-    owned_blocks = bundle[:, : seats_per_row * block_len].reshape(seat_blocks.shape)
     owned_cols = bundle[:, seats_per_row * block_len : seats_per_row * block_len + seats_per_row, 0]
     owned_cols = owned_cols.astype(jnp.int32)
     hidden = to_grid(states)
@@ -134,7 +136,7 @@
                 axis=-1,
             )
         hidden, mixed = couple_step(
-            pieces_all, owned_blocks, owned_cols, hidden, mix_weight, gain, bias
+            pieces_all, bundle, owned_cols, hidden, mix_weight, gain, bias, iteration + 1 < ITERS
         )
     return to_grid(hidden)
 

time: 177 us -> 176 us (level)
  transfers between devices with their start and end apart: 2 -> 2, of which waited for: 1 -> 1; matrix products, arithmetic and copies ran while one was open for 5% -> 4% of each run, Pallas kernels for 0% -> 0%
where the time goes in v8:
time: 176 us
  blocking collectives  97 us (55%)
  waiting for transfers between devices  30 us (17%)
  between operations  14.1 us (8%)
  Pallas kernels  12.2 us (7%)
  local copies, waits for them, and re-layouts  8.44 us (5%)
  starting transfers between devices  7.44 us (4%)
  other arithmetic  4.84 us (3%)
  matrix products  1.85 us (1%)
    all_to_all x2, blocking collectives, to_grid(): lax.all_to_all(values, 'col', split_axis=0, concat_axis=0, tiled=True)  59.5 us
    all_to_all x1, waiting for transfers between devices, body(): lax.all_to_all(bundle, 'row', split_axis=0, concat_axis=0, tiled=True)  29.9 us
    all_gather x1, blocking collectives, body(): lax.all_gather(mixed[:, :half], 'row', axis=0, tiled=False)  19 us
    all_gather x1, blocking collectives, body(): lax.all_gather(mixed[:, half:], 'row', axis=0, tiled=False)  18.5 us
    pallas_call x2, Pallas kernels, couple_step(): pl.pallas_call(couple_kernel, out_shape=tuple((jax.ShapeDtypeStruct(hidde...  12.2 us
    all_to_all x1, starting transfers between devices, body(): lax.all_to_all(bundle, 'row', split_axis=0, concat_axis=0, tiled=True)  7.44 us
  transfers between devices with their start and end apart: 2, of which 1 were waited for; matrix products, arithmetic and copies ran while one was open for 4% of the time, Pallas kernels for 0%

profile of v8, /device:TPU:2, one launch (start us, length us, event | category | flops | bytes accessed | tf_op | source)
XLA Modules:
  0.0 175.9 jit_solution(15856164720190460457)
XLA Ops:
  6.5 0.0 copy-start.1
  6.5 0.0 all-gather.5.cloned.1.call-start
  6.5 1.0 all_to_all.19
  7.6 35.7 %all_to_all.28 = bf16[64,2,384]{2,1,0:T(2,128)(2,1)S(1)} all-to-all(bf16[64,2,384]{2,1,0:T(2,128)(2,1)S(1)} %all_to_all.19), channel_id=1, replica_groups=mesh['row'=16,'col'=64] {'col'}, dimensions={0} | all-to-all | bytes 196608 | tf_op jit(solution)/shard_map/all_to_all | solution.py:20
  43.3 0.0 copy-start.2
  43.3 1.8 %convolution_convert_fusion = bf16[128,384]{1,0:T(8,128)(2,1)} fusion(bf16[128,384]{1,0:T(8,128)(2,1)S(1)} %all_to_all.21.hidden_ref, bf16[384,384]{1,0:T(8,128)(2,1)} %weight_ref.3), kind=kOutput, calls=%fused_computation.5 | convolution fusion | flops 37797888 | bytes 491520 | tf_op jit(solution)/shard_map/dot_general | solution.py:125
  45.1 0.0 all-gather.5.cloned.1.call-update
  45.8 0.9 convert_reduce_fusion.1
  46.7 0.7 fusion.4
  47.4 0.8 scatter_custom_fusion.1
  48.2 0.1 convert_element_type.27
  48.3 0.2 broadcast_in_dim.8
  48.5 0.0 copy-done.1
  48.6 1.8 %scatter_fusion = bf16[32,128,128]{2,1,0:T(8,128)(2,1)S(1)} fusion(bf16[32,128,128]{2,1,0:T(8,128)(2,1)S(1)} %broadcast_in_dim.8, s32[32]{0:T(128)S(1)} %fusion.4, bf16[32,128,128]{2,1,0:T(8,128)(2,1)S(1)} %bitcast.30), kind=kCustom, calls=%fused_computation | custom fusion | bytes 3145856 | tf_op jit(solution)/shard_map/scatter | solution.py:39
  50.3 0.0 copy-done.2
  50.4 0.1 broadcast_in_dim.10
  50.4 1.1 fusion.1
  51.5 0.0 copy-start.3
  51.5 0.0 copy-start.4
  51.5 7.4 %all-to-all-start = ((bf16[16,272,128]{2,1,0:T(8,128)(2,1)}), bf16[16,272,128]{2,1,0:T(8,128)(2,1)S(1)}, u32[]{:S(2)}, u32[]{:S(2)}) async-start(bf16[16,272,128]{2,1,0:T(8,128)(2,1)} %fusion.1), calls=%async_computation | async-start | bytes 2228224 | tf_op jit(solution)/shard_map/all_to_all | solution.py:121
  59.0 0.0 copy-done.3
  59.0 0.6 reshape.68.gain_ref
  59.6 0.0 copy-done.4
  59.6 0.5 reshape.69.bias_ref
  60.1 29.9 %all-to-all-done.bundle_ref = bf16[16,272,128]{2,1,0:T(8,128)(2,1)S(1)} async-done(((bf16[16,272,128]{2,1,0:T(8,128)(2,1)}), bf16[16,272,128]{2,1,0:T(8,128)(2,1)S(1)}, u32[]{:S(2)}, u32[]{:S(2)}) %all-to-all-start) | async-done | bytes 1114144 | tf_op jit(solution)/shard_map/all_to_all | solution.py:121
  90.1 0.0 copy-start
  90.1 0.3 convert_reduce_fusion
  90.4 0.6 reshape.70.cols_ref
  91.0 0.0 all-gather.5.cloned.1.call-done
  91.0 0.0 copy-done
  91.1 6.2 %shard_map.82 = (bf16[128,384]{1,0:T(8,128)(2,1)}, bf16[128,384]{1,0:T(8,128)(2,1)}) custom-call(s32[32]{0:T(128)} %reshape.70.cols_ref, bf16[16,272,128]{2,1,0:T(8,128)(2,1)} %copy-done, bf16[16,128,384]{2,1,0:T(8,128)(2,1)} %bitcast.29, bf16[128,384]{1,0:T(8,128)(2,1)} %copy-done.2, bf16[384,384]{1,0:T(8,128)(2,1)} %weight_ref.3, ...), custom_call_target="tpu_custom_call" | custom-call | tf_op jit(solution)/shard_map/pallas_call | solution.py:84
  97.2 1.0 fusion.7
  98.2 19.0 %all-gather.1 = bf16[2048,192]{1,0:T(8,128)(2,1)S(1)} all-gather(bf16[128,192]{1,0:T(8,128)(2,1)S(1)} %get-tuple-element.9), channel_id=3, replica_groups=mesh['row'=16,'col'=64] {'row'}, dimensions={0}, use_global_device_ids=true | all-gather | bytes 835584 | tf_op jit(solution)/shard_map/all_gather | solution.py:133
  117.2 18.5 %all-gather.2 = bf16[2048,192]{1,0:T(8,128)(2,1)S(1)} all-gather(bf16[128,192]{1,0:T(8,128)(2,1)S(1)} %get-tuple-element.10), channel_id=4, replica_groups=mesh['row'=16,'col'=64] {'row'}, dimensions={0}, use_global_device_ids=true | all-gather | bytes 835584 | tf_op jit(solution)/shard_map/all_gather | solution.py:134
  135.8 1.8 %pad_maximum_fusion.pieces_ref = bf16[16,128,384]{2,1,0:T(8,128)(2,1)} fusion(bf16[16,128,192]{2,1,0:T(8,128)(2,1)S(1)} %bitcast.28, bf16[16,128,192]{2,1,0:T(8,128)(2,1)S(1)} %bitcast.27), kind=kLoop, calls=%fused_computation.4 | loop fusion | flops 3145728 | bytes 3145728 | tf_op jit(solution)/shard_map/concatenate | solution.py:131
  137.6 6.0 %shard_map.83 = bf16[128,384]{1,0:T(8,128)(2,1)} custom-call(s32[32]{0:T(128)} %reshape.70.cols_ref, bf16[16,272,128]{2,1,0:T(8,128)(2,1)} %copy-done, bf16[16,128,384]{2,1,0:T(8,128)(2,1)} %pad_maximum_fusion.pieces_ref, bf16[128,384]{1,0:T(8,128)(2,1)} %get-tuple-element.8.hidden_ref, bf16[384,384]{1,0:T(8,128)(2,1)} %weight_ref.3, ...), custom_call_target="tpu_custom_call" | custom-call | tf_op jit(solution)/shard_map/pallas_call | solution.py:84
  143.6 0.9 all_to_all.22
  144.5 23.8 %all_to_all.29 = bf16[64,2,384]{2,1,0:T(2,128)(2,1)S(1)} all-to-all(bf16[64,2,384]{2,1,0:T(2,128)(2,1)S(1)} %all_to_all.22), channel_id=1, replica_groups=mesh['row'=16,'col'=64] {'col'}, dimensions={0} | all-to-all | bytes 196608 | tf_op jit(solution)/shard_map/all_to_all | solution.py:20
  168.4 0.7 all_to_all.24
  (3 shorter events, 0.1 us)
Async XLA Ops:
  6.5 42.0 %copy-start.1 = (bf16[1,1,32,128,128]{4,3,2,1,0:T(8,128)(2,1)S(1)}, bf16[1,1,32,128,128]{4,3,2,1,0:T(8,128)(2,1)}, u32[]{:S(2)}) copy-start(bf16[1,1,32,128,128]{4,3,2,1,0:T(8,128)(2,1)} %param.10) | copy-start | bytes 3145732
  6.5 84.5 %all-gather.5.cloned.1.call-start = ((), (), s32[]{:S(2)}) async-start(), calls=%async_computation.3 | async-start | bytes 1671168 | tf_op jit(solution)/shard_map/all_gather | solution.py:128
  43.3 7.1 %copy-start.2 = (bf16[128,384]{1,0:T(8,128)(2,1)}, bf16[128,384]{1,0:T(8,128)(2,1)S(1)}, u32[]{:S(2)}) copy-start(bf16[128,384]{1,0:T(8,128)(2,1)S(1)} %all_to_all.21.hidden_ref) | copy-start | bytes 294916
  51.5 7.4 %copy-start.3 = (f32[384]{0:T(512)S(1)}, f32[384]{0:T(512)}, u32[]{:S(2)}) copy-start(f32[384]{0:T(512)} %param.14) | copy-start | bytes 4612
  51.5 8.0 %copy-start.4 = (f32[384]{0:T(512)S(1)}, f32[384]{0:T(512)}, u32[]{:S(2)}) copy-start(f32[384]{0:T(512)} %param.15) | copy-start | bytes 4612
  51.5 38.5 %all-to-all-start = ((bf16[16,272,128]{2,1,0:T(8,128)(2,1)}), bf16[16,272,128]{2,1,0:T(8,128)(2,1)S(1)}, u32[]{:S(2)}, u32[]{:S(2)}) async-start(bf16[16,272,128]{2,1,0:T(8,128)(2,1)} %fusion.1), calls=%async_computation | async-start | bytes 2228224 | tf_op jit(solution)/shard_map/all_to_all | solution.py:121
  90.1 1.0 copy-start
Sparse Core Ops, SparseCore 0:
  45.3 44.6 all-gather.4

commit v9 on v8

--- a/solution.py
+++ b/solution.py
@@ -69,7 +69,9 @@
             term = product if term is None else term + product
         return total + term.astype(jnp.bfloat16).astype(jnp.float32)
 
-    coupled = lax.fori_loop(0, sources, source_term, jnp.zeros(hidden_ref.shape, jnp.float32))
+    coupled = lax.fori_loop(
+        0, sources, source_term, jnp.zeros(hidden_ref.shape, jnp.float32), unroll=True
+    )
     hidden = normalize(hidden_ref[...], coupled, gain_ref[...], bias_ref[...])
     hidden_out[...] = hidden
     for out in mixed_out:

time: 176 us -> 172 us (0.977)
  Pallas kernels: 12.2 us -> 7.42 us
    pallas_call x2, Pallas kernels: 12.2 us -> 7.42 us  [couple_step(): pl.pallas_call(couple_kernel, out_shape=tuple((jax.ShapeDtypeStruct(hidde...]
  transfers between devices with their start and end apart: 2 -> 2, of which waited for: 1 -> 1; matrix products, arithmetic and copies ran while one was open for 4% -> 5% of each run, Pallas kernels for 0% -> 0%
where the time goes in v9:
time: 172 us; the launch traced here: 171 us
  blocking collectives  97.1 us (56%)
  waiting for transfers between devices  30 us (17%)
  between operations  14.1 us (8%)
  local copies, waits for them, and re-layouts  8.44 us (5%)
  starting transfers between devices  7.42 us (4%)
  Pallas kernels  7.42 us (4%)
  other arithmetic  4.84 us (3%)
  matrix products  1.85 us (1%)
    all_to_all x2, blocking collectives, to_grid(): lax.all_to_all(values, 'col', split_axis=0, concat_axis=0, tiled=True)  59.6 us
    all_to_all x1, waiting for transfers between devices, body(): lax.all_to_all(bundle, 'row', split_axis=0, concat_axis=0, tiled=True)  30 us
    all_gather x1, blocking collectives, body(): lax.all_gather(mixed[:, :half], 'row', axis=0, tiled=False)  18.9 us
    all_gather x1, blocking collectives, body(): lax.all_gather(mixed[:, half:], 'row', axis=0, tiled=False)  18.5 us
    pallas_call x2, Pallas kernels, couple_step(): pl.pallas_call(couple_kernel, out_shape=tuple((jax.ShapeDtypeStruct(hidde...  7.42 us
    all_to_all x1, starting transfers between devices, body(): lax.all_to_all(bundle, 'row', split_axis=0, concat_axis=0, tiled=True)  7.42 us
  transfers between devices with their start and end apart: 2, of which 1 were waited for; matrix products, arithmetic and copies ran while one was open for 5% of the time, Pallas kernels for 0%

profile of v9, /device:TPU:2, one launch (start us, length us, event | category | flops | bytes accessed | tf_op | source)
XLA Modules:
  0.0 171.2 jit_solution(17948803656043396327)
XLA Ops:
  6.5 0.0 copy-start.1
  6.5 0.0 all-gather.5.cloned.1.call-start
  6.5 1.0 all_to_all.19
  7.6 35.7 %all_to_all.28 = bf16[64,2,384]{2,1,0:T(2,128)(2,1)S(1)} all-to-all(bf16[64,2,384]{2,1,0:T(2,128)(2,1)S(1)} %all_to_all.19), channel_id=1, replica_groups=mesh['row'=16,'col'=64] {'col'}, dimensions={0} | all-to-all | bytes 196608 | tf_op jit(solution)/shard_map/all_to_all | solution.py:20
  43.3 0.0 copy-start.2
  43.3 1.8 %convolution_convert_fusion = bf16[128,384]{1,0:T(8,128)(2,1)} fusion(bf16[128,384]{1,0:T(8,128)(2,1)S(1)} %all_to_all.21.hidden_ref, bf16[384,384]{1,0:T(8,128)(2,1)} %weight_ref.3), kind=kOutput, calls=%fused_computation.5 | convolution fusion | flops 37797888 | bytes 491520 | tf_op jit(solution)/shard_map/dot_general | solution.py:127
  45.1 0.0 all-gather.5.cloned.1.call-update
  45.8 0.9 convert_reduce_fusion.1
  46.7 0.7 fusion.4
  47.4 0.8 scatter_custom_fusion.1
  48.2 0.1 convert_element_type.27
  48.3 0.2 broadcast_in_dim.8
  48.5 0.0 copy-done.1
  48.6 1.8 %scatter_fusion = bf16[32,128,128]{2,1,0:T(8,128)(2,1)S(1)} fusion(bf16[32,128,128]{2,1,0:T(8,128)(2,1)S(1)} %broadcast_in_dim.8, s32[32]{0:T(128)S(1)} %fusion.4, bf16[32,128,128]{2,1,0:T(8,128)(2,1)S(1)} %bitcast.30), kind=kCustom, calls=%fused_computation | custom fusion | bytes 3145856 | tf_op jit(solution)/shard_map/scatter | solution.py:39
  50.3 0.0 copy-done.2
  50.4 0.1 broadcast_in_dim.10
  50.4 1.1 fusion.1
  51.5 0.0 copy-start.3
  51.5 0.0 copy-start.4
  51.5 7.4 %all-to-all-start = ((bf16[16,272,128]{2,1,0:T(8,128)(2,1)}), bf16[16,272,128]{2,1,0:T(8,128)(2,1)S(1)}, u32[]{:S(2)}, u32[]{:S(2)}) async-start(bf16[16,272,128]{2,1,0:T(8,128)(2,1)} %fusion.1), calls=%async_computation | async-start | bytes 2228224 | tf_op jit(solution)/shard_map/all_to_all | solution.py:123
  58.9 0.0 copy-done.3
  59.0 0.6 reshape.68.gain_ref
  59.5 0.0 copy-done.4
  59.5 0.5 reshape.69.bias_ref
  60.1 30.0 %all-to-all-done.bundle_ref = bf16[16,272,128]{2,1,0:T(8,128)(2,1)S(1)} async-done(((bf16[16,272,128]{2,1,0:T(8,128)(2,1)}), bf16[16,272,128]{2,1,0:T(8,128)(2,1)S(1)}, u32[]{:S(2)}, u32[]{:S(2)}) %all-to-all-start) | async-done | bytes 1114144 | tf_op jit(solution)/shard_map/all_to_all | solution.py:123
  90.1 0.0 copy-start
  90.1 0.3 convert_reduce_fusion
  90.4 0.6 reshape.70.cols_ref
  91.1 0.0 all-gather.5.cloned.1.call-done
  91.1 0.0 copy-done
  91.1 3.8 %shard_map.82 = (bf16[128,384]{1,0:T(8,128)(2,1)}, bf16[128,384]{1,0:T(8,128)(2,1)}) custom-call(s32[32]{0:T(128)} %reshape.70.cols_ref, bf16[16,272,128]{2,1,0:T(8,128)(2,1)} %copy-done, bf16[16,128,384]{2,1,0:T(8,128)(2,1)} %bitcast.29, bf16[128,384]{1,0:T(8,128)(2,1)} %copy-done.2, bf16[384,384]{1,0:T(8,128)(2,1)} %weight_ref.3, ...), custom_call_target="tpu_custom_call" | custom-call | tf_op jit(solution)/shard_map/pallas_call | solution.py:86
  94.9 1.0 fusion.7
  95.9 18.9 %all-gather.1 = bf16[2048,192]{1,0:T(8,128)(2,1)S(1)} all-gather(bf16[128,192]{1,0:T(8,128)(2,1)S(1)} %get-tuple-element.9), channel_id=3, replica_groups=mesh['row'=16,'col'=64] {'row'}, dimensions={0}, use_global_device_ids=true | all-gather | bytes 835584 | tf_op jit(solution)/shard_map/all_gather | solution.py:135
  114.8 18.5 %all-gather.2 = bf16[2048,192]{1,0:T(8,128)(2,1)S(1)} all-gather(bf16[128,192]{1,0:T(8,128)(2,1)S(1)} %get-tuple-element.10), channel_id=4, replica_groups=mesh['row'=16,'col'=64] {'row'}, dimensions={0}, use_global_device_ids=true | all-gather | bytes 835584 | tf_op jit(solution)/shard_map/all_gather | solution.py:136
  133.3 1.8 %pad_maximum_fusion.pieces_ref = bf16[16,128,384]{2,1,0:T(8,128)(2,1)} fusion(bf16[16,128,192]{2,1,0:T(8,128)(2,1)S(1)} %bitcast.28, bf16[16,128,192]{2,1,0:T(8,128)(2,1)S(1)} %bitcast.27), kind=kLoop, calls=%fused_computation.4 | loop fusion | flops 3145728 | bytes 3145728 | tf_op jit(solution)/shard_map/concatenate | solution.py:133
  135.2 3.6 %shard_map.83 = bf16[128,384]{1,0:T(8,128)(2,1)} custom-call(s32[32]{0:T(128)} %reshape.70.cols_ref, bf16[16,272,128]{2,1,0:T(8,128)(2,1)} %copy-done, bf16[16,128,384]{2,1,0:T(8,128)(2,1)} %pad_maximum_fusion.pieces_ref, bf16[128,384]{1,0:T(8,128)(2,1)} %get-tuple-element.8.hidden_ref, bf16[384,384]{1,0:T(8,128)(2,1)} %weight_ref.3, ...), custom_call_target="tpu_custom_call" | custom-call | tf_op jit(solution)/shard_map/pallas_call | solution.py:86
  138.8 0.9 all_to_all.22
  139.7 24.0 %all_to_all.29 = bf16[64,2,384]{2,1,0:T(2,128)(2,1)S(1)} all-to-all(bf16[64,2,384]{2,1,0:T(2,128)(2,1)S(1)} %all_to_all.22), channel_id=1, replica_groups=mesh['row'=16,'col'=64] {'col'}, dimensions={0} | all-to-all | bytes 196608 | tf_op jit(solution)/shard_map/all_to_all | solution.py:20
  163.7 0.7 all_to_all.24
  (3 shorter events, 0.1 us)
Async XLA Ops:
  6.5 42.0 %copy-start.1 = (bf16[1,1,32,128,128]{4,3,2,1,0:T(8,128)(2,1)S(1)}, bf16[1,1,32,128,128]{4,3,2,1,0:T(8,128)(2,1)}, u32[]{:S(2)}) copy-start(bf16[1,1,32,128,128]{4,3,2,1,0:T(8,128)(2,1)} %param.10) | copy-start | bytes 3145732
  6.5 84.5 %all-gather.5.cloned.1.call-start = ((), (), s32[]{:S(2)}) async-start(), calls=%async_computation.3 | async-start | bytes 1671168 | tf_op jit(solution)/shard_map/all_gather | solution.py:130
  43.3 7.1 %copy-start.2 = (bf16[128,384]{1,0:T(8,128)(2,1)}, bf16[128,384]{1,0:T(8,128)(2,1)S(1)}, u32[]{:S(2)}) copy-start(bf16[128,384]{1,0:T(8,128)(2,1)S(1)} %all_to_all.21.hidden_ref) | copy-start | bytes 294916
  51.5 7.4 %copy-start.3 = (f32[384]{0:T(512)S(1)}, f32[384]{0:T(512)}, u32[]{:S(2)}) copy-start(f32[384]{0:T(512)} %param.14) | copy-start | bytes 4612
  51.5 8.0 %copy-start.4 = (f32[384]{0:T(512)S(1)}, f32[384]{0:T(512)}, u32[]{:S(2)}) copy-start(f32[384]{0:T(512)} %param.15) | copy-start | bytes 4612
  51.5 38.5 %all-to-all-start = ((bf16[16,272,128]{2,1,0:T(8,128)(2,1)}), bf16[16,272,128]{2,1,0:T(8,128)(2,1)S(1)}, u32[]{:S(2)}, u32[]{:S(2)}) async-start(bf16[16,272,128]{2,1,0:T(8,128)(2,1)} %fusion.1), calls=%async_computation | async-start | bytes 2228224 | tf_op jit(solution)/shard_map/all_to_all | solution.py:123
  90.1 1.0 copy-start
Sparse Core Ops, SparseCore 0:
  45.3 44.5 all-gather.4

commit v10 on v9

--- a/solution.py
+++ b/solution.py
@@ -61,12 +61,14 @@
     seats = cols_ref.shape[0] // sources
 
     def source_term(source, total):
-        term = None
-        for seat in range(seats):
-            piece = pieces_ref[cols_ref[source * seats + seat]]
-            block = bundle_ref[source, seat * block_len:(seat + 1) * block_len, :]
-            product = jnp.dot(block, piece, preferred_element_type=jnp.float32)
-            term = product if term is None else term + product
+        block = jnp.concatenate(
+            [bundle_ref[source, seat * block_len:(seat + 1) * block_len, :] for seat in range(seats)],
+            axis=1,
+        )
+        piece = jnp.concatenate(
+            [pieces_ref[cols_ref[source * seats + seat]] for seat in range(seats)], axis=0
+        )
+        term = jnp.dot(block, piece, preferred_element_type=jnp.float32)
         return total + term.astype(jnp.bfloat16).astype(jnp.float32)
 
     coupled = lax.fori_loop(

time: 172 us -> 171 us (level)
  no operation moved by 1% of the time
where the time goes in v10:
time: 171 us
  blocking collectives  97 us (57%)
  waiting for transfers between devices  30 us (18%)
  between operations  14.1 us (8%)
  local copies, waits for them, and re-layouts  8.44 us (5%)
  starting transfers between devices  7.45 us (4%)
  Pallas kernels  6.87 us (4%)
  other arithmetic  4.84 us (3%)
  matrix products  1.85 us (1%)
    all_to_all x2, blocking collectives, to_grid(): lax.all_to_all(values, 'col', split_axis=0, concat_axis=0, tiled=True)  59.5 us
    all_to_all x1, waiting for transfers between devices, body(): lax.all_to_all(bundle, 'row', split_axis=0, concat_axis=0, tiled=True)  29.9 us
    all_gather x1, blocking collectives, body(): lax.all_gather(mixed[:, :half], 'row', axis=0, tiled=False)  19 us
    all_gather x1, blocking collectives, body(): lax.all_gather(mixed[:, half:], 'row', axis=0, tiled=False)  18.5 us
    all_to_all x1, starting transfers between devices, body(): lax.all_to_all(bundle, 'row', split_axis=0, concat_axis=0, tiled=True)  7.45 us
    pallas_call x2, Pallas kernels, couple_step(): pl.pallas_call(couple_kernel, out_shape=tuple((jax.ShapeDtypeStruct(hidde...  6.87 us
  transfers between devices with their start and end apart: 2, of which 1 were waited for; matrix products, arithmetic and copies ran while one was open for 5% of the time, Pallas kernels for 0%

profile of v10, /device:TPU:2, one launch (start us, length us, event | category | flops | bytes accessed | tf_op | source)
XLA Modules:
  0.0 170.5 jit_solution(4899347508883850616)
XLA Ops:
  6.5 0.0 copy-start.1
  6.5 0.0 all-gather.5.cloned.1.call-start
  6.5 1.0 all_to_all.19
  7.6 35.7 %all_to_all.28 = bf16[64,2,384]{2,1,0:T(2,128)(2,1)S(1)} all-to-all(bf16[64,2,384]{2,1,0:T(2,128)(2,1)S(1)} %all_to_all.19), channel_id=1, replica_groups=mesh['row'=16,'col'=64] {'col'}, dimensions={0} | all-to-all | bytes 196608 | tf_op jit(solution)/shard_map/all_to_all | solution.py:20
  43.3 0.0 copy-start.2
  43.3 1.8 %convolution_convert_fusion = bf16[128,384]{1,0:T(8,128)(2,1)} fusion(bf16[128,384]{1,0:T(8,128)(2,1)S(1)} %all_to_all.21.hidden_ref, bf16[384,384]{1,0:T(8,128)(2,1)} %weight_ref.3), kind=kOutput, calls=%fused_computation.5 | convolution fusion | flops 37797888 | bytes 491520 | tf_op jit(solution)/shard_map/dot_general | solution.py:129
  45.1 0.0 all-gather.5.cloned.1.call-update
  45.8 0.9 convert_reduce_fusion.1
  46.7 0.7 fusion.4
  47.4 0.8 scatter_custom_fusion.1
  48.2 0.1 convert_element_type.27
  48.3 0.2 broadcast_in_dim.8
  48.5 0.0 copy-done.1
  48.6 1.8 %scatter_fusion = bf16[32,128,128]{2,1,0:T(8,128)(2,1)S(1)} fusion(bf16[32,128,128]{2,1,0:T(8,128)(2,1)S(1)} %broadcast_in_dim.8, s32[32]{0:T(128)S(1)} %fusion.4, bf16[32,128,128]{2,1,0:T(8,128)(2,1)S(1)} %bitcast.30), kind=kCustom, calls=%fused_computation | custom fusion | bytes 3145856 | tf_op jit(solution)/shard_map/scatter | solution.py:39
  50.3 0.0 copy-done.2
  50.3 0.1 broadcast_in_dim.10
  50.4 1.1 fusion.1
  51.5 0.0 copy-start.3
  51.5 0.0 copy-start.4
  51.5 7.4 %all-to-all-start = ((bf16[16,272,128]{2,1,0:T(8,128)(2,1)}), bf16[16,272,128]{2,1,0:T(8,128)(2,1)S(1)}, u32[]{:S(2)}, u32[]{:S(2)}) async-start(bf16[16,272,128]{2,1,0:T(8,128)(2,1)} %fusion.1), calls=%async_computation | async-start | bytes 2228224 | tf_op jit(solution)/shard_map/all_to_all | solution.py:125
  59.0 0.0 copy-done.3
  59.0 0.6 reshape.68.gain_ref
  59.6 0.0 copy-done.4
  59.6 0.5 reshape.69.bias_ref
  60.1 29.9 %all-to-all-done.bundle_ref = bf16[16,272,128]{2,1,0:T(8,128)(2,1)S(1)} async-done(((bf16[16,272,128]{2,1,0:T(8,128)(2,1)}), bf16[16,272,128]{2,1,0:T(8,128)(2,1)S(1)}, u32[]{:S(2)}, u32[]{:S(2)}) %all-to-all-start) | async-done | bytes 1114144 | tf_op jit(solution)/shard_map/all_to_all | solution.py:125
  90.1 0.0 copy-start
  90.1 0.3 convert_reduce_fusion
  90.4 0.6 reshape.70.cols_ref
  91.0 0.0 all-gather.5.cloned.1.call-done
  91.0 0.0 copy-done
  91.1 3.5 %shard_map.82 = (bf16[128,384]{1,0:T(8,128)(2,1)}, bf16[128,384]{1,0:T(8,128)(2,1)}) custom-call(s32[32]{0:T(128)} %reshape.70.cols_ref, bf16[16,272,128]{2,1,0:T(8,128)(2,1)} %copy-done, bf16[16,128,384]{2,1,0:T(8,128)(2,1)} %bitcast.29, bf16[128,384]{1,0:T(8,128)(2,1)} %copy-done.2, bf16[384,384]{1,0:T(8,128)(2,1)} %weight_ref.3, ...), custom_call_target="tpu_custom_call" | custom-call | tf_op jit(solution)/shard_map/pallas_call | solution.py:88
  94.6 1.0 fusion.7
  95.6 19.0 %all-gather.1 = bf16[2048,192]{1,0:T(8,128)(2,1)S(1)} all-gather(bf16[128,192]{1,0:T(8,128)(2,1)S(1)} %get-tuple-element.9), channel_id=3, replica_groups=mesh['row'=16,'col'=64] {'row'}, dimensions={0}, use_global_device_ids=true | all-gather | bytes 835584 | tf_op jit(solution)/shard_map/all_gather | solution.py:137
  114.6 18.5 %all-gather.2 = bf16[2048,192]{1,0:T(8,128)(2,1)S(1)} all-gather(bf16[128,192]{1,0:T(8,128)(2,1)S(1)} %get-tuple-element.10), channel_id=4, replica_groups=mesh['row'=16,'col'=64] {'row'}, dimensions={0}, use_global_device_ids=true | all-gather | bytes 835584 | tf_op jit(solution)/shard_map/all_gather | solution.py:138
  133.1 1.8 %pad_maximum_fusion.pieces_ref = bf16[16,128,384]{2,1,0:T(8,128)(2,1)} fusion(bf16[16,128,192]{2,1,0:T(8,128)(2,1)S(1)} %bitcast.28, bf16[16,128,192]{2,1,0:T(8,128)(2,1)S(1)} %bitcast.27), kind=kLoop, calls=%fused_computation.4 | loop fusion | flops 3145728 | bytes 3145728 | tf_op jit(solution)/shard_map/concatenate | solution.py:135
  134.9 3.4 %shard_map.83 = bf16[128,384]{1,0:T(8,128)(2,1)} custom-call(s32[32]{0:T(128)} %reshape.70.cols_ref, bf16[16,272,128]{2,1,0:T(8,128)(2,1)} %copy-done, bf16[16,128,384]{2,1,0:T(8,128)(2,1)} %pad_maximum_fusion.pieces_ref, bf16[128,384]{1,0:T(8,128)(2,1)} %get-tuple-element.8.hidden_ref, bf16[384,384]{1,0:T(8,128)(2,1)} %weight_ref.3, ...), custom_call_target="tpu_custom_call" | custom-call | tf_op jit(solution)/shard_map/pallas_call | solution.py:88
  138.3 0.9 all_to_all.22
  139.2 23.8 %all_to_all.29 = bf16[64,2,384]{2,1,0:T(2,128)(2,1)S(1)} all-to-all(bf16[64,2,384]{2,1,0:T(2,128)(2,1)S(1)} %all_to_all.22), channel_id=1, replica_groups=mesh['row'=16,'col'=64] {'col'}, dimensions={0} | all-to-all | bytes 196608 | tf_op jit(solution)/shard_map/all_to_all | solution.py:20
  163.0 0.7 all_to_all.24
  (3 shorter events, 0.1 us)
Async XLA Ops:
  6.5 42.0 %copy-start.1 = (bf16[1,1,32,128,128]{4,3,2,1,0:T(8,128)(2,1)S(1)}, bf16[1,1,32,128,128]{4,3,2,1,0:T(8,128)(2,1)}, u32[]{:S(2)}) copy-start(bf16[1,1,32,128,128]{4,3,2,1,0:T(8,128)(2,1)} %param.10) | copy-start | bytes 3145732
  6.5 84.5 %all-gather.5.cloned.1.call-start = ((), (), s32[]{:S(2)}) async-start(), calls=%async_computation.3 | async-start | bytes 1671168 | tf_op jit(solution)/shard_map/all_gather | solution.py:132
  43.3 7.1 %copy-start.2 = (bf16[128,384]{1,0:T(8,128)(2,1)}, bf16[128,384]{1,0:T(8,128)(2,1)S(1)}, u32[]{:S(2)}) copy-start(bf16[128,384]{1,0:T(8,128)(2,1)S(1)} %all_to_all.21.hidden_ref) | copy-start | bytes 294916
  51.5 7.5 %copy-start.3 = (f32[384]{0:T(512)S(1)}, f32[384]{0:T(512)}, u32[]{:S(2)}) copy-start(f32[384]{0:T(512)} %param.14) | copy-start | bytes 4612
  51.5 8.0 %copy-start.4 = (f32[384]{0:T(512)S(1)}, f32[384]{0:T(512)}, u32[]{:S(2)}) copy-start(f32[384]{0:T(512)} %param.15) | copy-start | bytes 4612
  51.5 38.5 %all-to-all-start = ((bf16[16,272,128]{2,1,0:T(8,128)(2,1)}), bf16[16,272,128]{2,1,0:T(8,128)(2,1)S(1)}, u32[]{:S(2)}, u32[]{:S(2)}) async-start(bf16[16,272,128]{2,1,0:T(8,128)(2,1)} %fusion.1), calls=%async_computation | async-start | bytes 2228224 | tf_op jit(solution)/shard_map/all_to_all | solution.py:125
  90.1 1.0 copy-start
Sparse Core Ops, SparseCore 0:
  45.3 44.6 all-gather.4
